TPU v7x, 768 devices: a whole 4x8x12 slice. The times are simulated.
768 devices in a mesh: lat: 48 (over z_lo, x, core), lon: 16 (over y, z_hi).
Axes of the slice: x: 4, y: 8, z: 12 (z_hi: 2, z_lo: 6; z = z_hi * 6 + z_lo), core: 2. Of those that a mesh axis runs over, the one named last changes fastest.
Arguments:
- tracers: float32 [3, 1, 768, 6144], P(None, None, 'lat', 'lon'), may hold values from -6 to 6
- lon_offsets: int32 [768], P('lat'), may hold values from -190 to 190, as said below
- lon_weights: float32 [4, 768], P(None, 'lat'), may hold values from -0.25 to 0.75
- lat_offsets: int32 [768], replicated, may hold values from -4 to 4, as said below
- lat_weights: float32 [4, 768], replicated, may hold values from -0.25 to 0.75
Outputs:
- advected: float32 [3, 1, 768, 6144], P(None, None, 'lat', 'lon')
Inputs may be any that keep to these rules, and one draw needn't show every extreme that they name: `lon_offsets`: magnitudes are larger in the polar quarters of the rows; the bound is reached in every draw. `lat_offsets`: the bound is reached in every draw.
All inputs are finite; a program needn't handle non-finite values.
Results may differ from a plain program's by a relative error of at most 0.0003.
Values sent between devices are 32-bit elements; how exact they have to be, the bound alone decides.
No kernel may reach another device: no remote copies, remote signals or barrier semaphores. Data moves between devices by JAX's collectives and lax.ppermute only.
A program may use at most 64 MiB of HBM per device.

v0:
```python
import jax
import jax.numpy as jnp
from jax import lax
from jax.sharding import PartitionSpec as P


def padded_2(block, sides, width):
    for axis, dim in sides:
        count = lax.axis_size(axis)
        forward = [(i, i + 1) for i in range(count - 1)]
        forward.append((count - 1, 0))
        backward = [(target, source) for source, target in forward]
        low = lax.ppermute(
            lax.slice_in_dim(block, block.shape[dim] - width, None, axis=dim), axis, forward
        )
        high = lax.ppermute(lax.slice_in_dim(block, 0, width, axis=dim), axis, backward)
        block = jnp.concatenate([low, block, high], axis=dim)
    return block


def row_taps(row, shift, taps, base, length):
    total = jnp.zeros(row.shape[:-1] + (length,), jnp.float32)
    for k in range(4):
        start = base - shift - 1 + k
        total = total + taps[k] * lax.dynamic_slice_in_dim(row, start, length, axis=row.ndim - 1)
    return total


def per_device(tracers, lon_offsets, lon_weights, lat_offsets, lat_weights):
    width = tracers.shape[3]
    reach = width // 2
    nlat = lat_offsets.shape[0]
    padded = padded_2(tracers, (("lon", 3),), reach)
    swept = jax.vmap(
        lambda r, s, w: row_taps(r, s, w, reach, width), in_axes=(2, 0, 1), out_axes=2
    )(padded, lon_offsets, lon_weights)
    every_row = jnp.arange(nlat, dtype=jnp.int32)
    turned = jnp.swapaxes(swept, 2, 3)
    block = lax.all_to_all(turned, "lat", split_axis=2, concat_axis=3, tiled=True)
    total = jnp.zeros(block.shape, jnp.float32)
    for k in range(4):
        source = jnp.clip(every_row - lat_offsets - 1 + k, 0, nlat - 1)
        total = total + lat_weights[k][None, :] * jnp.take(block, source, axis=3)
    returned = lax.all_to_all(total, "lat", split_axis=3, concat_axis=2, tiled=True)
    return jnp.swapaxes(returned, 2, 3)


def solution(mesh):
    return jax.shard_map(
        per_device,
        mesh=mesh,
        in_specs=(P(None, None, "lat", "lon"), P("lat"), P(None, "lat"), P(), P()),
        out_specs=P(None, None, "lat", "lon"),
        check_vma=False,
    )
```

profile of v0, /device:TPU:1, one launch (start us, length us, event | category | flops | bytes accessed | tf_op | source)
XLA Modules:
  0.0 148.4 jit_solution(12415872040270078308)
XLA Ops:
  0.0 0.9 fusion.19
  0.9 15.7 %collective-permute-start = (f32[3,1,16,192]{3,2,1,0:T(8,128)S(1)}, f32[3,1,16,192]{3,2,1,0:T(8,128)S(1)}, u32[]{:S(2)}, u32[]{:S(2)}) collective-permute-start(f32[3,1,16,192]{3,2,1,0:T(8,128)S(1)} %get-tuple-element.10), channel_id=1, source_target_pairs={{0,1},{1,2},{2,3},{3,4},{4,5},{5,6},{6,7},{7,8},{8,9},{9,10},{10,1... | collective-permute-start | bytes 110600 | tf_op jit(solution)/shard_map/ppermute | solution.py:13
  16.6 4.8 %collective-permute-start.1 = (f32[3,1,16,192]{3,2,1,0:T(8,128)S(1)}, f32[3,1,16,192]{3,2,1,0:T(8,128)S(1)}, u32[]{:S(2)}, u32[]{:S(2)}) collective-permute-start(f32[3,1,16,192]{3,2,1,0:T(8,128)S(1)} %get-tuple-element.11), channel_id=1, source_target_pairs={{1,0},{2,1},{3,2},{4,3},{5,4},{6,5},{7,6},{8,7},{9,8},{10,9},{11,1... | collective-permute-start | bytes 110600 | tf_op jit(solution)/shard_map/ppermute | solution.py:16
  21.5 0.7 fusion.18
  22.1 0.8 slice_bitcast_fusion.3
  23.0 0.7 compare_select_fusion.3
  23.7 0.9 slice_reduce_fusion.3
  24.6 0.0 collective-permute-done
  24.6 3.3 %collective-permute-done.1 = f32[3,1,16,192]{3,2,1,0:T(8,128)S(1)} collective-permute-done((f32[3,1,16,192]{3,2,1,0:T(8,128)S(1)}, f32[3,1,16,192]{3,2,1,0:T(8,128)S(1)}, u32[]{:S(2)}, u32[]{:S(2)}) %collective-permute-start.1) | collective-permute-done | bytes 36896 | tf_op jit(solution)/shard_map/ppermute | solution.py:16
  27.9 1.0 pad_maximum_fusion
  28.9 6.7 %copy.43 = f32[3,1,16,768]{0,1,2,3:T(1,128)} copy(f32[3,1,16,768]{3,2,1,0:T(8,128)S(1)} %pad_maximum_fusion) | data formatting | bytes 294912 | tf_op jit(solution)/shard_map/concatenate | solution.py:17
  35.5 6.6 %gather_fusion = f32[16,3,384]{1,0,2:T(8,128)} fusion(f32[16,3,1,768]{1,2,0,3:T(1,128)} %bitcast.115, s32[16]{0:T(128)S(1)} %get-tuple-element.24), kind=kCustom, calls=%fused_computation.4 | custom fusion | bytes 147712 | tf_op jit(solution)/shard_map/vmap()/gather | solution.py:25
  42.1 6.6 %gather_fusion.1 = f32[16,3,384]{1,0,2:T(8,128)} fusion(f32[16,3,1,768]{1,2,0,3:T(1,128)} %bitcast.116, s32[16]{0:T(128)S(1)} %get-tuple-element.25), kind=kCustom, calls=%fused_computation.5 | custom fusion | bytes 147712 | tf_op jit(solution)/shard_map/vmap()/gather | solution.py:25
  48.6 6.5 %gather_fusion.2 = f32[16,3,384]{1,0,2:T(8,128)} fusion(f32[16,3,1,768]{1,2,0,3:T(1,128)} %bitcast.117, s32[16]{0:T(128)S(1)} %get-tuple-element.27), kind=kCustom, calls=%fused_computation.6 | custom fusion | bytes 147712 | tf_op jit(solution)/shard_map/vmap()/gather | solution.py:25
  55.2 6.6 %gather_fusion.3 = f32[16,3,384]{1,0,2:T(8,128)} fusion(f32[16,3,1,768]{1,2,0,3:T(1,128)} %bitcast.118, s32[16]{0:T(128)S(1)} %get-tuple-element.26), kind=kCustom, calls=%fused_computation.7 | custom fusion | bytes 147712 | tf_op jit(solution)/shard_map/vmap()/gather | solution.py:25
  61.7 5.5 %fusion.1 = f32[3,1,384,16]{0,3,2,1:T(8,128)S(1)} fusion(f32[16,3,384]{1,0,2:T(8,128)} %gather_fusion.3, f32[16,3,384]{1,0,2:T(8,128)} %gather_fusion.2, f32[16,3,384]{1,0,2:T(8,128)} %gather_fusion.1, f32[16,3,384]{1,0,2:T(8,128)} %gather_fusion, f32[16]{0:T(128)S(1)} %get-tuple-element.22, f32[16]{0:T(128)S(1)} %get-tuple-element.23, ...), kind=kLoop, calls=%fused_computation.10 | loop fusion | flops 129024 | bytes 368896 | tf_op jit(solution)/shard_map/transpose;vmap()/transpose | solution.py:38
  67.3 0.0 copy-start
  67.3 3.4 %copy.44 = f32[3,1,384,16]{3,1,0,2:T(1,128)} copy(f32[3,1,384,16]{0,3,2,1:T(8,128)S(1)} %fusion.1) | data formatting | bytes 147456 | tf_op jit(solution)/shard_map/transpose;vmap()/transpose | solution.py:38
  70.6 0.5 broadcast.329
  71.2 3.3 %reduce.8 = f32[384,3,16]{2,1,0:T(4,128)S(1)} reduce(f32[384,3,1,16]{3,2,1,0:T(1,128)} %bitcast.121, f32[]{:T(128)} %broadcast.329), dimensions={2}, to_apply=%bitcast.109.reduce_sub_computation | reduce | bytes 147460
  74.5 1.1 reshape.193
  75.6 12.1 %all-to-all-start = ((f32[48,1,384]{2,1,0:T(1,128)}), f32[48,1,384]{2,1,0:T(1,128)S(1)}, u32[]{:S(2)}, u32[]{:S(2)}) async-start(f32[48,1,384]{2,1,0:T(1,128)} %reshape.193), calls=%async_computation | async-start | bytes 147456 | tf_op jit(solution)/shard_map/all_to_all | solution.py:39
  87.8 0.0 copy-done
  87.8 11.0 %all-to-all-done = f32[48,1,384]{2,1,0:T(1,128)S(1)} async-done(((f32[48,1,384]{2,1,0:T(1,128)}), f32[48,1,384]{2,1,0:T(1,128)S(1)}, u32[]{:S(2)}, u32[]{:S(2)}) %all-to-all-start) | async-done | bytes 73760 | tf_op jit(solution)/shard_map/all_to_all | solution.py:39
  98.8 0.8 reduce.9
  99.6 1.0 reshape.194
  100.7 0.8 copy.59
  101.5 3.4 %gather_fusion.4 = f32[768,3,8]{2,1,0:T(4,128)} fusion(f32[3,8,768]{1,0,2:T(4,128)S(1)} %bitcast.126, s32[1024]{0:T(1024)S(1)} %get-tuple-element.31), kind=kCustom, calls=%fused_computation.clone | custom fusion | bytes 150528 | tf_op jit(solution)/shard_map/jit(_take)/gather | solution.py:43
  104.9 1.5 %copy.48 = f32[768,3,8]{0,2,1:T(8,128)S(1)} copy(f32[768,3,8]{2,1,0:T(4,128)} %gather_fusion.4) | data formatting | bytes 147456 | tf_op jit(solution)/shard_map/jit(_take)/gather | solution.py:43
  106.5 3.5 %gather_fusion.5 = f32[768,3,8]{2,1,0:T(4,128)} fusion(f32[3,8,768]{1,0,2:T(4,128)S(1)} %bitcast.127, s32[1024]{0:T(1024)S(1)} %get-tuple-element.30), kind=kCustom, calls=%fused_computation.1.clone | custom fusion | bytes 150528 | tf_op jit(solution)/shard_map/jit(_take)/gather | solution.py:43
  110.0 1.5 %copy.50 = f32[768,3,8]{0,2,1:T(8,128)S(1)} copy(f32[768,3,8]{2,1,0:T(4,128)} %gather_fusion.5) | data formatting | bytes 147456 | tf_op jit(solution)/shard_map/jit(_take)/gather | solution.py:43
  111.5 3.5 %gather_fusion.6 = f32[768,3,8]{2,1,0:T(4,128)} fusion(f32[3,8,768]{1,0,2:T(4,128)S(1)} %bitcast.128, s32[1024]{0:T(1024)S(1)} %get-tuple-element.29), kind=kCustom, calls=%fused_computation.2.clone | custom fusion | bytes 150528 | tf_op jit(solution)/shard_map/jit(_take)/gather | solution.py:43
  115.0 1.5 %copy.52 = f32[768,3,8]{0,2,1:T(8,128)S(1)} copy(f32[768,3,8]{2,1,0:T(4,128)} %gather_fusion.6) | data formatting | bytes 147456 | tf_op jit(solution)/shard_map/jit(_take)/gather | solution.py:43
  116.5 3.5 %gather_fusion.7 = f32[768,3,8]{2,1,0:T(4,128)} fusion(f32[3,8,768]{1,0,2:T(4,128)S(1)} %bitcast.129, s32[1024]{0:T(1024)S(1)} %get-tuple-element.28), kind=kCustom, calls=%fused_computation.3.clone | custom fusion | bytes 150528 | tf_op jit(solution)/shard_map/jit(_take)/gather | solution.py:43
  120.0 1.5 %copy.54 = f32[768,3,8]{0,2,1:T(8,128)S(1)} copy(f32[768,3,8]{2,1,0:T(4,128)} %gather_fusion.7) | data formatting | bytes 147456 | tf_op jit(solution)/shard_map/jit(_take)/gather | solution.py:43
  121.5 0.1 fusion.5
  121.6 1.0 copy.55
  122.6 4.5 %reduce.10 = f32[768,3,8]{2,1,0:T(4,128)S(1)} reduce(f32[768,3,1,8]{3,2,1,0:T(1,128)S(1)} %bitcast.119, f32[]{:T(128)} %broadcast.329), dimensions={2}, to_apply=%bitcast.111.reduce_sub_computation | reduce | bytes 147460
  127.1 0.9 reshape.195
  128.0 15.1 %all_to_all.36 = f32[48,1,384]{2,1,0:T(1,128)S(1)} all-to-all(f32[48,1,384]{2,1,0:T(1,128)S(1)} %reshape.195), channel_id=1, replica_groups=mesh['lat'=48,'lon'=16] {'lat'}, dimensions={0} | all-to-all | bytes 147456 | tf_op jit(solution)/shard_map/all_to_all | solution.py:44
  143.1 0.8 reduce.11
  143.9 1.8 %reshape.196 = f32[768,3,1,8]{3,2,1,0:T(1,128)S(1)} reshape(f32[48,384]{1,0:T(8,128)S(1)} %reduce.11) | data formatting | bytes 147456
  145.7 1.4 copy.56
  147.1 0.2 all_to_all.31
  147.3 0.2 copy.63
  147.5 0.8 copy.58
  (4 shorter events, 0.1 us)
Async XLA Ops:
  0.9 23.6 %collective-permute-start = (f32[3,1,16,192]{3,2,1,0:T(8,128)S(1)}, f32[3,1,16,192]{3,2,1,0:T(8,128)S(1)}, u32[]{:S(2)}, u32[]{:S(2)}) collective-permute-start(f32[3,1,16,192]{3,2,1,0:T(8,128)S(1)} %get-tuple-element.10), channel_id=1, source_target_pairs={{0,1},{1,2},{2,3},{3,4},{4,5},{5,6},{6,7},{7,8},{8,9},{9,10},{10,1... | collective-permute-start | bytes 110600 | tf_op jit(solution)/shard_map/ppermute | solution.py:13
  16.6 11.2 %collective-permute-start.1 = (f32[3,1,16,192]{3,2,1,0:T(8,128)S(1)}, f32[3,1,16,192]{3,2,1,0:T(8,128)S(1)}, u32[]{:S(2)}, u32[]{:S(2)}) collective-permute-start(f32[3,1,16,192]{3,2,1,0:T(8,128)S(1)} %get-tuple-element.11), channel_id=1, source_target_pairs={{1,0},{2,1},{3,2},{4,3},{5,4},{6,5},{7,6},{8,7},{9,8},{10,9},{11,1... | collective-permute-start | bytes 110600 | tf_op jit(solution)/shard_map/ppermute | solution.py:16
  67.3 20.5 %copy-start = (s32[768]{0:T(1024)S(1)}, s32[768]{0:T(1024)}, u32[]{:S(2)}) copy-start(s32[768]{0:T(1024)} %param.10) | copy-start | bytes 9220
  75.6 23.2 %all-to-all-start = ((f32[48,1,384]{2,1,0:T(1,128)}), f32[48,1,384]{2,1,0:T(1,128)S(1)}, u32[]{:S(2)}, u32[]{:S(2)}) async-start(f32[48,1,384]{2,1,0:T(1,128)} %reshape.193), calls=%async_computation | async-start | bytes 147456 | tf_op jit(solution)/shard_map/all_to_all | solution.py:39
where the time goes:
time: 149 us; the launch traced here: 148 us
  local copies, waits for them, and re-layouts  68.9 us (46%)
  starting transfers between devices  32.6 us (22%)
  other arithmetic  17.4 us (12%)
  blocking collectives  15.1 us (10%)
  waiting for transfers between devices  14.3 us (10%)
    gather x4, local copies, waits for them, and re-layouts, row_taps(): lax.dynamic_slice_in_dim(row, start, length, axis=row.ndim - 1)  26.2 us
    gather x8, local copies, waits for them, and re-layouts, per_device(): total = total + lat_weights[k][None, :] * jnp.take(block, source, axis=3)  20 us
    ppermute x1, starting transfers between devices, padded_2(): lax.ppermute(lax.slice_in_dim(block, block.shape[dim] - width, None, axis...  15.7 us
    all_to_all x1, blocking collectives, per_device(): lax.all_to_all(total, 'lat', split_axis=3, concat_axis=2, tiled=True)  15.1 us
    all_to_all x1, starting transfers between devices, per_device(): lax.all_to_all(turned, 'lat', split_axis=2, concat_axis=3, tiled=True)  12.1 us
    all_to_all x1, waiting for transfers between devices, per_device(): lax.all_to_all(turned, 'lat', split_axis=2, concat_axis=3, tiled=True)  11 us
    unnamed x2, other arithmetic  7.83 us
    concatenate x1, local copies, waits for them, and re-layouts, padded_2(): block = jnp.concatenate([low, block, high], axis=dim)  6.68 us
  transfers between devices with their start and end apart: 3, of which 2 were waited for; matrix products, arithmetic and copies ran while one was open for 2% of the time, Pallas kernels for 0%

commit v1 on v0

v1 whole, which is shorter than its diff:
```python
import jax
import jax.numpy as jnp
from jax import lax
from jax.experimental import pallas as pl
from jax.experimental.pallas import tpu as pltpu
from jax.sharding import PartitionSpec as P

LON_HALO = 256
LAT_HALO = 8
SHIFT_BITS = 9
INTERPRET = False


def lon_kernel(left_ref, mid_ref, right_ref, base_ref, w_ref, out_ref, top_ref, bot_ref):
    tracers, rows, width = mid_ref.shape
    ext_width = width + 2 * LON_HALO
    base = base_ref[...]
    masks = [((base >> b) & 1) == 1 for b in range(SHIFT_BITS)]
    w = w_ref[...]
    for t in range(tracers):
        row = jnp.concatenate([left_ref[t], mid_ref[t], right_ref[t]], axis=1)
        for b in range(SHIFT_BITS):
            rolled = pltpu.roll(row, ext_width - (1 << b), 1)
            row = jnp.where(masks[b], rolled, row)
        total = jnp.zeros((rows, width), jnp.float32)
        for k in range(4):
            tap = row if k == 0 else pltpu.roll(row, ext_width - k, 1)
            total = total + w[:, k:k + 1] * tap[:, :width]
        out_ref[t] = total
        top_ref[t] = total[:LAT_HALO]
        bot_ref[t] = total[rows - LAT_HALO:]


def lat_kernel(up_ref, mid_ref, down_ref, d_ref, w_ref, out_ref):
    tracers, rows, width = mid_ref.shape
    ext_rows = rows + 2 * LAT_HALO
    d = d_ref[...]
    w = w_ref[...]
    for t in range(tracers):
        ext = jnp.concatenate([up_ref[t], mid_ref[t], down_ref[t]], axis=0)
        picks = [jnp.zeros((rows, width), jnp.float32) for _ in range(4)]
        for s in range(ext_rows - rows + 1):
            shifted = (ext if s == 0 else pltpu.roll(ext, ext_rows - s, 0))[:rows]
            for k in range(4):
                picks[k] = jnp.where(d[:, k:k + 1] == s, shifted, picks[k])
        total = jnp.zeros((rows, width), jnp.float32)
        for k in range(4):
            total = total + w[:, k:k + 1] * picks[k]
        out_ref[t] = total


def per_device(tracers, lon_offsets, lon_weights, lat_offsets, lat_weights):
    nt, nl, rows, width = tracers.shape
    block = tracers.reshape(nt * nl, rows, width)
    f32 = jnp.float32

    lon_count = lax.axis_size("lon")
    forward = [(i, (i + 1) % lon_count) for i in range(lon_count)]
    backward = [(b, a) for a, b in forward]
    left = lax.ppermute(block[:, :, width - LON_HALO:], "lon", forward)
    right = lax.ppermute(block[:, :, :LON_HALO], "lon", backward)

    base = (LON_HALO - lon_offsets - 1).astype(jnp.int32).reshape(rows, 1)
    lw = jnp.transpose(lon_weights).astype(f32)
    shape = jax.ShapeDtypeStruct((nt * nl, rows, width), f32)
    halo = jax.ShapeDtypeStruct((nt * nl, LAT_HALO, width), f32)
    swept, top, bot = pl.pallas_call(lon_kernel, out_shape=(shape, halo, halo), interpret=INTERPRET)(
        left, block, right, base, lw
    )

    lat_count = lax.axis_size("lat")
    down_pairs = [(i, i + 1) for i in range(lat_count - 1)]
    up_pairs = [(i + 1, i) for i in range(lat_count - 1)]
    up = lax.ppermute(bot, "lat", down_pairs)
    down = lax.ppermute(top, "lat", up_pairs)

    nlat = lat_offsets.shape[0]
    first = lax.axis_index("lat") * rows
    own = first + jnp.arange(rows, dtype=jnp.int32)
    offs = lax.dynamic_slice_in_dim(lat_offsets, first, rows)
    lat_w = lax.dynamic_slice_in_dim(lat_weights, first, rows, axis=1)
    taps = jnp.arange(4, dtype=jnp.int32)
    source = jnp.clip(own[:, None] - offs[:, None] - 1 + taps[None, :], 0, nlat - 1)
    d = (source - first + LAT_HALO - jnp.arange(rows, dtype=jnp.int32)[:, None]).astype(jnp.int32)
    out = pl.pallas_call(lat_kernel, out_shape=shape, interpret=INTERPRET)(
        up, swept, down, d, jnp.transpose(lat_w).astype(f32)
    )
    return out.reshape(tracers.shape)


def solution(mesh):
    return jax.shard_map(
        per_device,
        mesh=mesh,
        in_specs=(P(None, None, "lat", "lon"), P("lat"), P(None, "lat"), P(), P()),
        out_specs=P(None, None, "lat", "lon"),
        check_vma=False,
    )
```

time: 149 us -> 45.8 us (0.31)
  the two profiles are of different devices: /device:TPU:1 before, /device:TPU:223 now
where the time goes in v1:
time: 45.8 us; the launch traced here: 45.4 us
  starting transfers between devices  23 us (50%)
  waiting for transfers between devices  12.6 us (28%)
  local copies, waits for them, and re-layouts  4.22 us (9%)
  Pallas kernels  4.13 us (9%)
  other arithmetic  1.44 us (3%)
    ppermute x1, starting transfers between devices, per_device(): left = lax.ppermute(block[:, :, width - LON_HALO:], 'lon', forward)  12.1 us
    ppermute x1, starting transfers between devices, per_device(): up = lax.ppermute(bot, 'lat', down_pairs)  6.98 us
    ppermute x1, waiting for transfers between devices, per_device(): right = lax.ppermute(block[:, :, :LON_HALO], 'lon', backward)  6.5 us
    ppermute x1, waiting for transfers between devices, per_device(): down = lax.ppermute(top, 'lat', up_pairs)  6.11 us
    unnamed x16, local copies, waits for them, and re-layouts  2.59 us
    pallas_call x1, Pallas kernels, per_device(): pl.pallas_call(lon_kernel, out_shape=(shape, halo, halo), interpret=INTER...  2.24 us
    ppermute x1, starting transfers between devices, per_device(): right = lax.ppermute(block[:, :, :LON_HALO], 'lon', backward)  1.92 us
    ppermute x1, starting transfers between devices, per_device(): down = lax.ppermute(top, 'lat', up_pairs)  1.92 us
  transfers between devices with their start and end apart: 4, of which 2 were waited for; matrix products, arithmetic and copies ran while one was open for 8% of the time, Pallas kernels for 0%

profile of v1, /device:TPU:223, one launch (start us, length us, event | category | flops | bytes accessed | tf_op | source)
XLA Modules:
  0.0 45.4 jit_solution(241332570565856502)
XLA Ops:
  0.0 0.0 copy-start
  0.0 0.9 %fusion = (f32[3,16,256]{2,1,0:T(8,128)S(1)}, f32[3,16,256]{2,1,0:T(8,128)S(1)}) fusion(f32[3,16,384]{2,1,0:T(8,128)} %bitcast.8), kind=kLoop, calls=%fused_computation.4 | loop fusion | bytes 196608 | tf_op jit(solution)/shard_map/slice | solution.py:61
  0.9 12.1 %collective-permute-start = (f32[3,16,256]{2,1,0:T(8,128)S(1)}, f32[3,16,256]{2,1,0:T(8,128)S(1)}, u32[]{:S(2)}, u32[]{:S(2)}) collective-permute-start(f32[3,16,256]{2,1,0:T(8,128)S(1)} %get-tuple-element.12), channel_id=1, source_target_pairs={{0,1},{1,2},{2,3},{3,4},{4,5},{5,6},{6,7},{7,8},{8,9},{9,10},{10,1... | collective-permute-start | bytes 147464 | tf_op jit(solution)/shard_map/ppermute | solution.py:60
  13.0 1.9 %collective-permute-start.1 = (f32[3,16,256]{2,1,0:T(8,128)S(1)}, f32[3,16,256]{2,1,0:T(8,128)S(1)}, u32[]{:S(2)}, u32[]{:S(2)}) collective-permute-start(f32[3,16,256]{2,1,0:T(8,128)S(1)} %get-tuple-element.11), channel_id=1, source_target_pairs={{1,0},{2,1},{3,2},{4,3},{5,4},{6,5},{7,6},{8,7},{9,8},{10,9},{11,1... | collective-permute-start | bytes 147464 | tf_op jit(solution)/shard_map/ppermute | solution.py:61
  15.0 0.8 %subtract_add_fusion = s32[16]{0:T(128)S(1)} fusion(s32[768]{0:T(1024)} %param.8, s32[]{:T(128)S(6)} %select_n.4, s32[]{:T(128)S(6)} %mul.3), kind=kLoop, calls=%fused_computation.1 | loop fusion | flops 48 | bytes 136 | tf_op jit(solution)/shard_map/sub | solution.py:83
  15.8 0.0 copy-start.6
  15.8 0.7 %iota_subtract_fusion.d_ref = s32[16,4]{1,0:T(8,128)} fusion(s32[]{:T(128)S(6)} %mul.3, s32[16]{0:T(128)S(1)} %subtract_add_fusion), kind=kLoop, calls=%fused_computation | loop fusion | flops 320 | bytes 324 | tf_op jit(solution)/shard_map/sub | solution.py:84
  16.4 0.0 copy-done.6
  16.4 0.0 copy-start.5
  16.4 0.7 %copy.7.base_ref = s32[16,1]{1,0:T(8,128)} copy(s32[16,1]{0,1:T(1,128)S(1)} %subtract_bitcast_fusion) | data formatting | bytes 128 | tf_op jit(solution)/shard_map/reshape | solution.py:63
  17.1 0.0 copy-done.5
  17.1 0.7 %copy.6 = f32[4,16]{0,1:T(8,128)} copy(f32[4,16]{1,0:T(4,128)S(1)} %copy-done.5) | data formatting | bytes 512 | tf_op args[2]
  17.8 0.0 collective-permute-done.left_ref
  17.8 0.0 copy-start.1
  17.8 6.5 %collective-permute-done.1.right_ref = f32[3,16,256]{2,1,0:T(8,128)S(1)} collective-permute-done((f32[3,16,256]{2,1,0:T(8,128)S(1)}, f32[3,16,256]{2,1,0:T(8,128)S(1)}, u32[]{:S(2)}, u32[]{:S(2)}) %collective-permute-start.1) | collective-permute-done | bytes 49184 | tf_op jit(solution)/shard_map/ppermute | solution.py:61
  24.3 0.0 copy-start.2
  24.3 0.0 copy-done.1
  24.3 0.6 %copy-done.2 = f32[3,16,256]{2,1,0:T(8,128)} copy-done((f32[3,16,256]{2,1,0:T(8,128)}, f32[3,16,256]{2,1,0:T(8,128)S(1)}, u32[]{:S(2)}) %copy-start.2) | copy-done | bytes 49176
  24.9 2.2 %shard_map.55 = (f32[3,16,384]{2,1,0:T(8,128)}, f32[3,8,384]{2,1,0:T(8,128)}, f32[3,8,384]{2,1,0:T(8,128)}) custom-call(f32[3,16,256]{2,1,0:T(8,128)} %copy-done.1, f32[3,16,384]{2,1,0:T(8,128)} %bitcast.9, f32[3,16,256]{2,1,0:T(8,128)} %copy-done.2, s32[16,1]{1,0:T(8,128)} %copy.7.base_ref, f32[16,4]{1,0:T(8,128)} %bitcast.10), custom_call_target="tpu_custom_call" | custom-call | tf_op jit(solution)/shard_map/pallas_call | solution.py:67
  27.1 7.0 %collective-permute-start.2 = (f32[3,8,384]{2,1,0:T(8,128)}, f32[3,8,384]{2,1,0:T(8,128)S(1)}, u32[]{:S(2)}, u32[]{:S(2)}) collective-permute-start(f32[3,8,384]{2,1,0:T(8,128)} %get-tuple-element.8), channel_id=1, source_target_pairs={{0,16},{16,32},{32,48},{48,64},{64,80},{80,96},{96,112},{112,128},... | collective-permute-start | bytes 110600 | tf_op jit(solution)/shard_map/ppermute | solution.py:74
  34.1 1.9 %collective-permute-start.3 = (f32[3,8,384]{2,1,0:T(8,128)}, f32[3,8,384]{2,1,0:T(8,128)S(1)}, u32[]{:S(2)}, u32[]{:S(2)}) collective-permute-start(f32[3,8,384]{2,1,0:T(8,128)} %get-tuple-element.10), channel_id=1, source_target_pairs={{16,0},{32,16},{48,32},{64,48},{80,64},{96,80},{112,96},{128,112},... | collective-permute-start | bytes 110600 | tf_op jit(solution)/shard_map/ppermute | solution.py:75
  36.1 0.0 copy-done
  36.1 0.1 constant_dynamic-slice_fusion
  36.1 0.7 %copy.10 = f32[4,16]{0,1:T(8,128)} copy(f32[4,16]{1,0:T(4,128)S(1)} %constant_dynamic-slice_fusion) | data formatting | bytes 512
  36.8 0.0 collective-permute-done.2.up_ref
  36.8 0.0 copy-start.3
  36.8 6.1 %collective-permute-done.3.down_ref = f32[3,8,384]{2,1,0:T(8,128)S(1)} collective-permute-done((f32[3,8,384]{2,1,0:T(8,128)}, f32[3,8,384]{2,1,0:T(8,128)S(1)}, u32[]{:S(2)}, u32[]{:S(2)}) %collective-permute-start.3) | collective-permute-done | bytes 36896 | tf_op jit(solution)/shard_map/ppermute | solution.py:75
  42.9 0.0 copy-start.4
  42.9 0.0 copy-done.3
  42.9 0.6 %copy-done.4 = f32[3,8,384]{2,1,0:T(8,128)} copy-done((f32[3,8,384]{2,1,0:T(8,128)}, f32[3,8,384]{2,1,0:T(8,128)S(1)}, u32[]{:S(2)}) %copy-start.4) | copy-done | bytes 36888
  43.6 1.9 %shard_map.56 = f32[3,16,384]{2,1,0:T(8,128)} custom-call(f32[3,8,384]{2,1,0:T(8,128)} %copy-done.3, f32[3,16,384]{2,1,0:T(8,128)} %get-tuple-element.9.mid_ref, f32[3,8,384]{2,1,0:T(8,128)} %copy-done.4, s32[16,4]{1,0:T(8,128)} %iota_subtract_fusion.d_ref, f32[16,4]{1,0:T(8,128)} %bitcast.11), custom_call_target="tpu_custom_call" | custom-call | tf_op jit(solution)/shard_map/pallas_call | solution.py:85
  (1 shorter events, 0.0 us)
Async XLA Ops:
  0.0 36.1 %copy-start = (f32[4,768]{1,0:T(4,128)S(1)}, f32[4,768]{1,0:T(4,128)}, u32[]{:S(2)}) copy-start(f32[4,768]{1,0:T(4,128)} %param.9) | copy-start | bytes 36868
  0.9 16.9 %collective-permute-start = (f32[3,16,256]{2,1,0:T(8,128)S(1)}, f32[3,16,256]{2,1,0:T(8,128)S(1)}, u32[]{:S(2)}, u32[]{:S(2)}) collective-permute-start(f32[3,16,256]{2,1,0:T(8,128)S(1)} %get-tuple-element.12), channel_id=1, source_target_pairs={{0,1},{1,2},{2,3},{3,4},{4,5},{5,6},{6,7},{7,8},{8,9},{9,10},{10,1... | collective-permute-start | bytes 147464 | tf_op jit(solution)/shard_map/ppermute | solution.py:60
  13.0 11.2 %collective-permute-start.1 = (f32[3,16,256]{2,1,0:T(8,128)S(1)}, f32[3,16,256]{2,1,0:T(8,128)S(1)}, u32[]{:S(2)}, u32[]{:S(2)}) collective-permute-start(f32[3,16,256]{2,1,0:T(8,128)S(1)} %get-tuple-element.11), channel_id=1, source_target_pairs={{1,0},{2,1},{3,2},{4,3},{5,4},{6,5},{7,6},{8,7},{9,8},{10,9},{11,1... | collective-permute-start | bytes 147464 | tf_op jit(solution)/shard_map/ppermute | solution.py:61
  15.8 0.7 %copy-start.6 = (s32[16]{0:T(128)S(1)}, s32[16]{0:T(128)}, u32[]{:S(2)}) copy-start(s32[16]{0:T(128)} %param.6) | copy-start | bytes 196
  16.4 0.7 %copy-start.5 = (f32[4,16]{1,0:T(4,128)S(1)}, f32[4,16]{1,0:T(4,128)}, u32[]{:S(2)}) copy-start(f32[4,16]{1,0:T(4,128)} %param.7) | copy-start | bytes 772
  17.8 6.5 %copy-start.1 = (f32[3,16,256]{2,1,0:T(8,128)}, f32[3,16,256]{2,1,0:T(8,128)S(1)}, u32[]{:S(2)}) copy-start(f32[3,16,256]{2,1,0:T(8,128)S(1)} %collective-permute-done.left_ref) | copy-start | bytes 147460
  24.3 0.6 %copy-start.2 = (f32[3,16,256]{2,1,0:T(8,128)}, f32[3,16,256]{2,1,0:T(8,128)S(1)}, u32[]{:S(2)}) copy-start(f32[3,16,256]{2,1,0:T(8,128)S(1)} %collective-permute-done.1.right_ref) | copy-start | bytes 147460
  27.1 9.7 %collective-permute-start.2 = (f32[3,8,384]{2,1,0:T(8,128)}, f32[3,8,384]{2,1,0:T(8,128)S(1)}, u32[]{:S(2)}, u32[]{:S(2)}) collective-permute-start(f32[3,8,384]{2,1,0:T(8,128)} %get-tuple-element.8), channel_id=1, source_target_pairs={{0,16},{16,32},{32,48},{48,64},{64,80},{80,96},{96,112},{112,128},... | collective-permute-start | bytes 110600 | tf_op jit(solution)/shard_map/ppermute | solution.py:74
  34.1 8.8 %collective-permute-start.3 = (f32[3,8,384]{2,1,0:T(8,128)}, f32[3,8,384]{2,1,0:T(8,128)S(1)}, u32[]{:S(2)}, u32[]{:S(2)}) collective-permute-start(f32[3,8,384]{2,1,0:T(8,128)} %get-tuple-element.10), channel_id=1, source_target_pairs={{16,0},{32,16},{48,32},{64,48},{80,64},{96,80},{112,96},{128,112},... | collective-permute-start | bytes 110600 | tf_op jit(solution)/shard_map/ppermute | solution.py:75
  36.8 6.1 %copy-start.3 = (f32[3,8,384]{2,1,0:T(8,128)}, f32[3,8,384]{2,1,0:T(8,128)S(1)}, u32[]{:S(2)}) copy-start(f32[3,8,384]{2,1,0:T(8,128)S(1)} %collective-permute-done.2.up_ref) | copy-start | bytes 110596
  42.9 0.6 %copy-start.4 = (f32[3,8,384]{2,1,0:T(8,128)}, f32[3,8,384]{2,1,0:T(8,128)S(1)}, u32[]{:S(2)}) copy-start(f32[3,8,384]{2,1,0:T(8,128)S(1)} %collective-permute-done.3.down_ref) | copy-start | bytes 110596

commit v2 on v1

--- a/solution.py
+++ b/solution.py
@@ -18,7 +18,9 @@
     masks = [((base >> b) & 1) == 1 for b in range(SHIFT_BITS)]
     w = w_ref[...]
     for t in range(tracers):
-        row = jnp.concatenate([left_ref[t], mid_ref[t], right_ref[t]], axis=1)
+        row = jnp.concatenate(
+            [left_ref[t, :, width - LON_HALO:], mid_ref[t], right_ref[t, :, :LON_HALO]], axis=1
+        )
         for b in range(SHIFT_BITS):
             rolled = pltpu.roll(row, ext_width - (1 << b), 1)
             row = jnp.where(masks[b], rolled, row)
@@ -49,6 +51,14 @@
         out_ref[t] = total
 
 
+def vmem_call(kernel, out_shape, count):
+    spec = pl.BlockSpec(memory_space=pltpu.VMEM)
+    outs = jax.tree_util.tree_map(lambda _: spec, out_shape)
+    return pl.pallas_call(
+        kernel, out_shape=out_shape, in_specs=[spec] * count, out_specs=outs, interpret=INTERPRET
+    )
+
+
 def per_device(tracers, lon_offsets, lon_weights, lat_offsets, lat_weights):
     nt, nl, rows, width = tracers.shape
     block = tracers.reshape(nt * nl, rows, width)
@@ -57,14 +67,14 @@
     lon_count = lax.axis_size("lon")
     forward = [(i, (i + 1) % lon_count) for i in range(lon_count)]
     backward = [(b, a) for a, b in forward]
-    left = lax.ppermute(block[:, :, width - LON_HALO:], "lon", forward)
-    right = lax.ppermute(block[:, :, :LON_HALO], "lon", backward)
+    left = lax.ppermute(block, "lon", forward)
+    right = lax.ppermute(block, "lon", backward)
 
     base = (LON_HALO - lon_offsets - 1).astype(jnp.int32).reshape(rows, 1)
     lw = jnp.transpose(lon_weights).astype(f32)
     shape = jax.ShapeDtypeStruct((nt * nl, rows, width), f32)
     halo = jax.ShapeDtypeStruct((nt * nl, LAT_HALO, width), f32)
-    swept, top, bot = pl.pallas_call(lon_kernel, out_shape=(shape, halo, halo), interpret=INTERPRET)(
+    swept, top, bot = vmem_call(lon_kernel, (shape, halo, halo), 5)(
         left, block, right, base, lw
     )
 
@@ -82,7 +92,7 @@
     taps = jnp.arange(4, dtype=jnp.int32)
     source = jnp.clip(own[:, None] - offs[:, None] - 1 + taps[None, :], 0, nlat - 1)
     d = (source - first + LAT_HALO - jnp.arange(rows, dtype=jnp.int32)[:, None]).astype(jnp.int32)
-    out = pl.pallas_call(lat_kernel, out_shape=shape, interpret=INTERPRET)(
+    out = vmem_call(lat_kernel, shape, 5)(
         up, swept, down, d, jnp.transpose(lat_w).astype(f32)
     )
     return out.reshape(tracers.shape)

time: 45.8 us -> 47.2 us (1.031)
  the two profiles are of different devices: /device:TPU:223 before, /device:TPU:31 now
where the time goes in v2:
time: 47.2 us; the launch traced here: 46.8 us
  starting transfers between devices  22.9 us (49%)
  waiting for transfers between devices  14.7 us (31%)
  Pallas kernels  4.23 us (9%)
  local copies, waits for them, and re-layouts  3.37 us (7%)
  other arithmetic  1.44 us (3%)
    ppermute x1, starting transfers between devices, per_device(): left = lax.ppermute(block, 'lon', forward)  15 us
    ppermute x1, waiting for transfers between devices, per_device(): right = lax.ppermute(block, 'lon', backward)  9.84 us
    ppermute x1, waiting for transfers between devices, per_device(): down = lax.ppermute(top, 'lat', up_pairs)  4.9 us
    ppermute x1, starting transfers between devices, per_device(): up = lax.ppermute(bot, 'lat', down_pairs)  4.11 us
    unnamed x16, local copies, waits for them, and re-layouts  2.62 us
    pallas_call x1, Pallas kernels, per_device(): vmem_call(lon_kernel, (shape, halo, halo), 5)(left, block, right, base, lw)  2.34 us
    ppermute x1, starting transfers between devices, per_device(): right = lax.ppermute(block, 'lon', backward)  1.92 us
    ppermute x1, starting transfers between devices, per_device(): down = lax.ppermute(top, 'lat', up_pairs)  1.92 us
  transfers between devices with their start and end apart: 4, of which 2 were waited for; matrix products, arithmetic and copies ran while one was open for 8% of the time, Pallas kernels for 0%

profile of v2, /device:TPU:31, one launch (start us, length us, event | category | flops | bytes accessed | tf_op | source)
XLA Modules:
  0.0 46.8 jit_solution(4629143565100928526)
XLA Ops:
  0.0 0.0 copy-start
  0.0 15.0 %collective-permute-start = (f32[3,16,384]{2,1,0:T(8,128)}, f32[3,16,384]{2,1,0:T(8,128)S(1)}, u32[]{:S(2)}, u32[]{:S(2)}) collective-permute-start(f32[3,16,384]{2,1,0:T(8,128)} %bitcast.8), channel_id=1, source_target_pairs={{0,1},{1,2},{2,3},{3,4},{4,5},{5,6},{6,7},{7,8},{8,9},{9,10},{10,1... | collective-permute-start | bytes 221192 | tf_op jit(solution)/shard_map/ppermute | solution.py:70
  15.0 1.9 %collective-permute-start.1 = (f32[3,16,384]{2,1,0:T(8,128)}, f32[3,16,384]{2,1,0:T(8,128)S(1)}, u32[]{:S(2)}, u32[]{:S(2)}) collective-permute-start(f32[3,16,384]{2,1,0:T(8,128)} %bitcast.9), channel_id=1, source_target_pairs={{1,0},{2,1},{3,2},{4,3},{5,4},{6,5},{7,6},{8,7},{9,8},{10,9},{11,1... | collective-permute-start | bytes 221192 | tf_op jit(solution)/shard_map/ppermute | solution.py:71
  16.9 0.8 %subtract_add_fusion = s32[16]{0:T(128)S(1)} fusion(s32[768]{0:T(1024)} %param.8, s32[]{:T(128)S(6)} %select_n.4, s32[]{:T(128)S(6)} %mul.3), kind=kLoop, calls=%fused_computation.1 | loop fusion | flops 48 | bytes 136 | tf_op jit(solution)/shard_map/sub | solution.py:93
  17.7 0.0 copy-start.6
  17.7 0.7 %iota_subtract_fusion.d_ref = s32[16,4]{1,0:T(8,128)} fusion(s32[]{:T(128)S(6)} %mul.3, s32[16]{0:T(128)S(1)} %subtract_add_fusion), kind=kLoop, calls=%fused_computation | loop fusion | flops 320 | bytes 324 | tf_op jit(solution)/shard_map/sub | solution.py:94
  18.4 0.0 copy-done.6
  18.4 0.0 copy-start.5
  18.4 0.7 %copy.7.base_ref = s32[16,1]{1,0:T(8,128)} copy(s32[16,1]{0,1:T(1,128)S(1)} %subtract_bitcast_fusion) | data formatting | bytes 128 | tf_op jit(solution)/shard_map/reshape | solution.py:73
  19.1 0.0 copy-done.5
  19.1 0.7 %copy.6 = f32[4,16]{0,1:T(8,128)} copy(f32[4,16]{1,0:T(4,128)S(1)} %copy-done.5) | data formatting | bytes 512 | tf_op args[2]
  19.7 0.0 collective-permute-done.left_ref
  19.7 0.0 copy-start.1
  19.7 9.8 %collective-permute-done.1.right_ref = f32[3,16,384]{2,1,0:T(8,128)S(1)} collective-permute-done((f32[3,16,384]{2,1,0:T(8,128)}, f32[3,16,384]{2,1,0:T(8,128)S(1)}, u32[]{:S(2)}, u32[]{:S(2)}) %collective-permute-start.1) | collective-permute-done | bytes 73760 | tf_op jit(solution)/shard_map/ppermute | solution.py:71
  29.6 0.0 copy-start.2
  29.6 0.0 copy-done.1
  29.6 0.6 %copy-done.2 = f32[3,16,384]{2,1,0:T(8,128)} copy-done((f32[3,16,384]{2,1,0:T(8,128)}, f32[3,16,384]{2,1,0:T(8,128)S(1)}, u32[]{:S(2)}) %copy-start.2) | copy-done | bytes 73752
  30.2 2.3 %shard_map.55 = (f32[3,16,384]{2,1,0:T(8,128)}, f32[3,8,384]{2,1,0:T(8,128)}, f32[3,8,384]{2,1,0:T(8,128)}) custom-call(f32[3,16,384]{2,1,0:T(8,128)} %copy-done.1, f32[3,16,384]{2,1,0:T(8,128)} %bitcast.10, f32[3,16,384]{2,1,0:T(8,128)} %copy-done.2, s32[16,1]{1,0:T(8,128)} %copy.7.base_ref, f32[16,4]{1,0:T(8,128)} %bitcast.12), custom_call_target="tpu_custom_call" | custom-call | tf_op jit(solution)/shard_map/pallas_call | solution.py:77
  32.6 4.1 %collective-permute-start.2 = (f32[3,8,384]{2,1,0:T(8,128)}, f32[3,8,384]{2,1,0:T(8,128)S(1)}, u32[]{:S(2)}, u32[]{:S(2)}) collective-permute-start(f32[3,8,384]{2,1,0:T(8,128)} %get-tuple-element.8), channel_id=1, source_target_pairs={{0,16},{16,32},{32,48},{48,64},{64,80},{80,96},{96,112},{112,128},... | collective-permute-start | bytes 110600 | tf_op jit(solution)/shard_map/ppermute | solution.py:84
  36.7 1.9 %collective-permute-start.3 = (f32[3,8,384]{2,1,0:T(8,128)}, f32[3,8,384]{2,1,0:T(8,128)S(1)}, u32[]{:S(2)}, u32[]{:S(2)}) collective-permute-start(f32[3,8,384]{2,1,0:T(8,128)} %get-tuple-element.10), channel_id=1, source_target_pairs={{16,0},{32,16},{48,32},{64,48},{80,64},{96,80},{112,96},{128,112},... | collective-permute-start | bytes 110600 | tf_op jit(solution)/shard_map/ppermute | solution.py:85
  38.6 0.0 copy-done
  38.6 0.1 constant_dynamic-slice_fusion
  38.7 0.7 %copy.10 = f32[4,16]{0,1:T(8,128)} copy(f32[4,16]{1,0:T(4,128)S(1)} %constant_dynamic-slice_fusion) | data formatting | bytes 512
  39.4 0.0 collective-permute-done.2.up_ref
  39.4 0.0 copy-start.3
  39.4 4.9 %collective-permute-done.3.down_ref = f32[3,8,384]{2,1,0:T(8,128)S(1)} collective-permute-done((f32[3,8,384]{2,1,0:T(8,128)}, f32[3,8,384]{2,1,0:T(8,128)S(1)}, u32[]{:S(2)}, u32[]{:S(2)}) %collective-permute-start.3) | collective-permute-done | bytes 36896 | tf_op jit(solution)/shard_map/ppermute | solution.py:85
  44.3 0.0 copy-start.4
  44.3 0.0 copy-done.3
  44.3 0.6 %copy-done.4 = f32[3,8,384]{2,1,0:T(8,128)} copy-done((f32[3,8,384]{2,1,0:T(8,128)}, f32[3,8,384]{2,1,0:T(8,128)S(1)}, u32[]{:S(2)}) %copy-start.4) | copy-done | bytes 36888
  44.9 1.9 %shard_map.56 = f32[3,16,384]{2,1,0:T(8,128)} custom-call(f32[3,8,384]{2,1,0:T(8,128)} %copy-done.3, f32[3,16,384]{2,1,0:T(8,128)} %get-tuple-element.9.mid_ref, f32[3,8,384]{2,1,0:T(8,128)} %copy-done.4, s32[16,4]{1,0:T(8,128)} %iota_subtract_fusion.d_ref, f32[16,4]{1,0:T(8,128)} %bitcast.11), custom_call_target="tpu_custom_call" | custom-call | tf_op jit(solution)/shard_map/pallas_call | solution.py:95
  (1 shorter events, 0.0 us)
Async XLA Ops:
  0.0 38.6 %copy-start = (f32[4,768]{1,0:T(4,128)S(1)}, f32[4,768]{1,0:T(4,128)}, u32[]{:S(2)}) copy-start(f32[4,768]{1,0:T(4,128)} %param.9) | copy-start | bytes 36868
  0.0 19.7 %collective-permute-start = (f32[3,16,384]{2,1,0:T(8,128)}, f32[3,16,384]{2,1,0:T(8,128)S(1)}, u32[]{:S(2)}, u32[]{:S(2)}) collective-permute-start(f32[3,16,384]{2,1,0:T(8,128)} %bitcast.8), channel_id=1, source_target_pairs={{0,1},{1,2},{2,3},{3,4},{4,5},{5,6},{6,7},{7,8},{8,9},{9,10},{10,1... | collective-permute-start | bytes 221192 | tf_op jit(solution)/shard_map/ppermute | solution.py:70
  15.0 14.6 %collective-permute-start.1 = (f32[3,16,384]{2,1,0:T(8,128)}, f32[3,16,384]{2,1,0:T(8,128)S(1)}, u32[]{:S(2)}, u32[]{:S(2)}) collective-permute-start(f32[3,16,384]{2,1,0:T(8,128)} %bitcast.9), channel_id=1, source_target_pairs={{1,0},{2,1},{3,2},{4,3},{5,4},{6,5},{7,6},{8,7},{9,8},{10,9},{11,1... | collective-permute-start | bytes 221192 | tf_op jit(solution)/shard_map/ppermute | solution.py:71
  17.7 0.7 %copy-start.6 = (s32[16]{0:T(128)S(1)}, s32[16]{0:T(128)}, u32[]{:S(2)}) copy-start(s32[16]{0:T(128)} %param.6) | copy-start | bytes 196
  18.4 0.7 %copy-start.5 = (f32[4,16]{1,0:T(4,128)S(1)}, f32[4,16]{1,0:T(4,128)}, u32[]{:S(2)}) copy-start(f32[4,16]{1,0:T(4,128)} %param.7) | copy-start | bytes 772
  19.7 9.8 %copy-start.1 = (f32[3,16,384]{2,1,0:T(8,128)}, f32[3,16,384]{2,1,0:T(8,128)S(1)}, u32[]{:S(2)}) copy-start(f32[3,16,384]{2,1,0:T(8,128)S(1)} %collective-permute-done.left_ref) | copy-start | bytes 221188
  29.6 0.6 %copy-start.2 = (f32[3,16,384]{2,1,0:T(8,128)}, f32[3,16,384]{2,1,0:T(8,128)S(1)}, u32[]{:S(2)}) copy-start(f32[3,16,384]{2,1,0:T(8,128)S(1)} %collective-permute-done.1.right_ref) | copy-start | bytes 221188
  32.6 6.8 %collective-permute-start.2 = (f32[3,8,384]{2,1,0:T(8,128)}, f32[3,8,384]{2,1,0:T(8,128)S(1)}, u32[]{:S(2)}, u32[]{:S(2)}) collective-permute-start(f32[3,8,384]{2,1,0:T(8,128)} %get-tuple-element.8), channel_id=1, source_target_pairs={{0,16},{16,32},{32,48},{48,64},{64,80},{80,96},{96,112},{112,128},... | collective-permute-start | bytes 110600 | tf_op jit(solution)/shard_map/ppermute | solution.py:84
  36.7 7.6 %collective-permute-start.3 = (f32[3,8,384]{2,1,0:T(8,128)}, f32[3,8,384]{2,1,0:T(8,128)S(1)}, u32[]{:S(2)}, u32[]{:S(2)}) collective-permute-start(f32[3,8,384]{2,1,0:T(8,128)} %get-tuple-element.10), channel_id=1, source_target_pairs={{16,0},{32,16},{48,32},{64,48},{80,64},{96,80},{112,96},{128,112},... | collective-permute-start | bytes 110600 | tf_op jit(solution)/shard_map/ppermute | solution.py:85
  39.4 4.9 %copy-start.3 = (f32[3,8,384]{2,1,0:T(8,128)}, f32[3,8,384]{2,1,0:T(8,128)S(1)}, u32[]{:S(2)}) copy-start(f32[3,8,384]{2,1,0:T(8,128)S(1)} %collective-permute-done.2.up_ref) | copy-start | bytes 110596
  44.3 0.6 %copy-start.4 = (f32[3,8,384]{2,1,0:T(8,128)}, f32[3,8,384]{2,1,0:T(8,128)S(1)}, u32[]{:S(2)}) copy-start(f32[3,8,384]{2,1,0:T(8,128)S(1)} %collective-permute-done.3.down_ref) | copy-start | bytes 110596

commit v3 on v2

--- a/solution.py
+++ b/solution.py
@@ -5,22 +5,20 @@
 from jax.experimental.pallas import tpu as pltpu
 from jax.sharding import PartitionSpec as P
 
-LON_HALO = 256
+LON_HALO = 192
 LAT_HALO = 8
 SHIFT_BITS = 9
 INTERPRET = False
 
 
-def lon_kernel(left_ref, mid_ref, right_ref, base_ref, w_ref, out_ref, top_ref, bot_ref):
-    tracers, rows, width = mid_ref.shape
-    ext_width = width + 2 * LON_HALO
+def lon_kernel(ext_ref, base_ref, w_ref, out_ref, top_ref, bot_ref):
+    tracers, rows, width = out_ref.shape
+    ext_width = ext_ref.shape[2]
     base = base_ref[...]
     masks = [((base >> b) & 1) == 1 for b in range(SHIFT_BITS)]
     w = w_ref[...]
     for t in range(tracers):
-        row = jnp.concatenate(
-            [left_ref[t, :, width - LON_HALO:], mid_ref[t], right_ref[t, :, :LON_HALO]], axis=1
-        )
+        row = ext_ref[t]
         for b in range(SHIFT_BITS):
             rolled = pltpu.roll(row, ext_width - (1 << b), 1)
             row = jnp.where(masks[b], rolled, row)
@@ -67,16 +65,15 @@
     lon_count = lax.axis_size("lon")
     forward = [(i, (i + 1) % lon_count) for i in range(lon_count)]
     backward = [(b, a) for a, b in forward]
-    left = lax.ppermute(block, "lon", forward)
-    right = lax.ppermute(block, "lon", backward)
+    left = lax.ppermute(block[:, :, width - LON_HALO:], "lon", forward)
+    right = lax.ppermute(block[:, :, :LON_HALO], "lon", backward)
+    ext = jnp.concatenate([left, block, right], axis=2)
 
     base = (LON_HALO - lon_offsets - 1).astype(jnp.int32).reshape(rows, 1)
     lw = jnp.transpose(lon_weights).astype(f32)
     shape = jax.ShapeDtypeStruct((nt * nl, rows, width), f32)
     halo = jax.ShapeDtypeStruct((nt * nl, LAT_HALO, width), f32)
-    swept, top, bot = vmem_call(lon_kernel, (shape, halo, halo), 5)(
-        left, block, right, base, lw
-    )
+    swept, top, bot = vmem_call(lon_kernel, (shape, halo, halo), 3)(ext, base, lw)
 
     lat_count = lax.axis_size("lat")
     down_pairs = [(i, i + 1) for i in range(lat_count - 1)]

time: 47.2 us -> 51 us (1.081)
  the two profiles are of different devices: /device:TPU:31 before, /device:TPU:7 now
where the time goes in v3:
time: 51 us; the launch traced here: 50.6 us
  starting transfers between devices  24.5 us (48%)
  waiting for transfers between devices  16 us (31%)
  Pallas kernels  4.11 us (8%)
  local copies, waits for them, and re-layouts  3.73 us (7%)
  other arithmetic  2.2 us (4%)
    ppermute x1, starting transfers between devices, per_device(): right = lax.ppermute(block[:, :, :LON_HALO], 'lon', backward)  17.8 us
    ppermute x1, waiting for transfers between devices, per_device(): left = lax.ppermute(block[:, :, width - LON_HALO:], 'lon', forward)  11.1 us
    ppermute x1, waiting for transfers between devices, per_device(): down = lax.ppermute(top, 'lat', up_pairs)  4.89 us
    ppermute x1, starting transfers between devices, per_device(): up = lax.ppermute(bot, 'lat', down_pairs)  2.93 us
    pallas_call x1, Pallas kernels, per_device(): vmem_call(lon_kernel, (shape, halo, halo), 3)(ext, base, lw)  2.22 us
    unnamed x14, local copies, waits for them, and re-layouts  1.99 us
    ppermute x1, starting transfers between devices, per_device(): left = lax.ppermute(block[:, :, width - LON_HALO:], 'lon', forward)  1.92 us
    ppermute x1, starting transfers between devices, per_device(): down = lax.ppermute(top, 'lat', up_pairs)  1.92 us
  transfers between devices with their start and end apart: 4, of which 2 were waited for; matrix products, arithmetic and copies ran while one was open for 7% of the time, Pallas kernels for 0%

profile of v3, /device:TPU:7, one launch (start us, length us, event | category | flops | bytes accessed | tf_op | source)
XLA Modules:
  0.0 50.6 jit_solution(5056576441169823300)
XLA Ops:
  0.0 0.0 copy-start
  0.0 0.0 copy-start.1
  0.0 1.0 %fusion = (f32[3,16,192]{2,1,0:T(8,128)S(1)}, f32[3,16,192]{2,1,0:T(8,128)S(1)}) fusion(f32[3,16,384]{2,1,0:T(8,128)} %bitcast.8), kind=kLoop, calls=%fused_computation.5 | loop fusion | bytes 147456 | tf_op jit(solution)/shard_map/slice | solution.py:68
  1.0 17.8 %collective-permute-start.1 = (f32[3,16,192]{2,1,0:T(8,128)S(1)}, f32[3,16,192]{2,1,0:T(8,128)S(1)}, u32[]{:S(2)}, u32[]{:S(2)}) collective-permute-start(f32[3,16,192]{2,1,0:T(8,128)S(1)} %get-tuple-element.12), channel_id=1, source_target_pairs={{1,0},{2,1},{3,2},{4,3},{5,4},{6,5},{7,6},{8,7},{9,8},{10,9},{11,1... | collective-permute-start | bytes 110600 | tf_op jit(solution)/shard_map/ppermute | solution.py:69
  18.8 1.9 %collective-permute-start = (f32[3,16,192]{2,1,0:T(8,128)S(1)}, f32[3,16,192]{2,1,0:T(8,128)S(1)}, u32[]{:S(2)}, u32[]{:S(2)}) collective-permute-start(f32[3,16,192]{2,1,0:T(8,128)S(1)} %get-tuple-element.11), channel_id=1, source_target_pairs={{0,1},{1,2},{2,3},{3,4},{4,5},{5,6},{6,7},{7,8},{8,9},{9,10},{10,1... | collective-permute-start | bytes 110600 | tf_op jit(solution)/shard_map/ppermute | solution.py:68
  20.7 0.8 %subtract_add_fusion = s32[16]{0:T(128)S(1)} fusion(s32[768]{0:T(1024)} %param.8, s32[]{:T(128)S(6)} %select_n.4, s32[]{:T(128)S(6)} %mul.3), kind=kLoop, calls=%fused_computation.2 | loop fusion | flops 48 | bytes 136 | tf_op jit(solution)/shard_map/sub | solution.py:90
  21.5 0.0 copy-start.5
  21.5 0.7 %iota_subtract_fusion.d_ref = s32[16,4]{1,0:T(8,128)} fusion(s32[]{:T(128)S(6)} %mul.3, s32[16]{0:T(128)S(1)} %subtract_add_fusion), kind=kLoop, calls=%fused_computation.1 | loop fusion | flops 320 | bytes 324 | tf_op jit(solution)/shard_map/sub | solution.py:91
  22.1 0.0 copy-done.5
  22.1 0.0 copy-start.4
  22.1 0.7 %copy.7.base_ref = s32[16,1]{1,0:T(8,128)} copy(s32[16,1]{0,1:T(1,128)S(1)} %subtract_bitcast_fusion) | data formatting | bytes 128 | tf_op jit(solution)/shard_map/reshape | solution.py:72
  22.8 0.0 copy-done.4
  22.8 0.7 %copy.6 = f32[4,16]{0,1:T(8,128)} copy(f32[4,16]{1,0:T(4,128)S(1)} %copy-done.4) | data formatting | bytes 512 | tf_op args[2]
  23.5 0.0 collective-permute-done.1
  23.5 11.1 %collective-permute-done = f32[3,16,192]{2,1,0:T(8,128)S(1)} collective-permute-done((f32[3,16,192]{2,1,0:T(8,128)S(1)}, f32[3,16,192]{2,1,0:T(8,128)S(1)}, u32[]{:S(2)}, u32[]{:S(2)}) %collective-permute-start) | collective-permute-done | bytes 36896 | tf_op jit(solution)/shard_map/ppermute | solution.py:68
  34.6 0.0 copy-done.1
  34.6 0.8 %pad_maximum_fusion.ext_ref = f32[3,16,768]{2,1,0:T(8,128)} fusion(f32[3,16,192]{2,1,0:T(8,128)S(1)} %collective-permute-done.1, f32[3,16,384]{2,1,0:T(8,128)S(1)} %bitcast.9, f32[3,16,192]{2,1,0:T(8,128)S(1)} %collective-permute-done), kind=kLoop, calls=%fused_computation | loop fusion | flops 73728 | bytes 294912 | tf_op jit(solution)/shard_map/concatenate | solution.py:70
  35.4 2.2 %shard_map.55 = (f32[3,16,384]{2,1,0:T(8,128)}, f32[3,8,384]{2,1,0:T(8,128)}, f32[3,8,384]{2,1,0:T(8,128)}) custom-call(f32[3,16,768]{2,1,0:T(8,128)} %pad_maximum_fusion.ext_ref, s32[16,1]{1,0:T(8,128)} %copy.7.base_ref, f32[16,4]{1,0:T(8,128)} %bitcast.10), custom_call_target="tpu_custom_call" | custom-call | tf_op jit(solution)/shard_map/pallas_call | solution.py:76
  37.6 2.9 %collective-permute-start.2 = (f32[3,8,384]{2,1,0:T(8,128)}, f32[3,8,384]{2,1,0:T(8,128)S(1)}, u32[]{:S(2)}, u32[]{:S(2)}) collective-permute-start(f32[3,8,384]{2,1,0:T(8,128)} %get-tuple-element.8), channel_id=1, source_target_pairs={{0,16},{16,32},{32,48},{48,64},{64,80},{80,96},{96,112},{112,128},... | collective-permute-start | bytes 110600 | tf_op jit(solution)/shard_map/ppermute | solution.py:81
  40.5 1.9 %collective-permute-start.3 = (f32[3,8,384]{2,1,0:T(8,128)}, f32[3,8,384]{2,1,0:T(8,128)S(1)}, u32[]{:S(2)}, u32[]{:S(2)}) collective-permute-start(f32[3,8,384]{2,1,0:T(8,128)} %get-tuple-element.10), channel_id=1, source_target_pairs={{16,0},{32,16},{48,32},{64,48},{80,64},{96,80},{112,96},{128,112},... | collective-permute-start | bytes 110600 | tf_op jit(solution)/shard_map/ppermute | solution.py:82
  42.4 0.0 copy-done
  42.5 0.1 constant_dynamic-slice_fusion
  42.5 0.7 %copy.10 = f32[4,16]{0,1:T(8,128)} copy(f32[4,16]{1,0:T(4,128)S(1)} %constant_dynamic-slice_fusion) | data formatting | bytes 512
  43.2 0.0 collective-permute-done.2.up_ref
  43.2 0.0 copy-start.2
  43.2 4.9 %collective-permute-done.3.down_ref = f32[3,8,384]{2,1,0:T(8,128)S(1)} collective-permute-done((f32[3,8,384]{2,1,0:T(8,128)}, f32[3,8,384]{2,1,0:T(8,128)S(1)}, u32[]{:S(2)}, u32[]{:S(2)}) %collective-permute-start.3) | collective-permute-done | bytes 36896 | tf_op jit(solution)/shard_map/ppermute | solution.py:82
  48.1 0.0 copy-start.3
  48.1 0.0 copy-done.2
  48.1 0.6 %copy-done.3 = f32[3,8,384]{2,1,0:T(8,128)} copy-done((f32[3,8,384]{2,1,0:T(8,128)}, f32[3,8,384]{2,1,0:T(8,128)S(1)}, u32[]{:S(2)}) %copy-start.3) | copy-done | bytes 36888
  48.7 1.9 %shard_map.56 = f32[3,16,384]{2,1,0:T(8,128)} custom-call(f32[3,8,384]{2,1,0:T(8,128)} %copy-done.2, f32[3,16,384]{2,1,0:T(8,128)} %get-tuple-element.9.mid_ref, f32[3,8,384]{2,1,0:T(8,128)} %copy-done.3, s32[16,4]{1,0:T(8,128)} %iota_subtract_fusion.d_ref, f32[16,4]{1,0:T(8,128)} %bitcast.11), custom_call_target="tpu_custom_call" | custom-call | tf_op jit(solution)/shard_map/pallas_call | solution.py:92
  (1 shorter events, 0.0 us)
Async XLA Ops:
  0.0 42.4 %copy-start = (f32[4,768]{1,0:T(4,128)S(1)}, f32[4,768]{1,0:T(4,128)}, u32[]{:S(2)}) copy-start(f32[4,768]{1,0:T(4,128)} %param.9) | copy-start | bytes 36868
  0.0 34.6 %copy-start.1 = (f32[3,1,16,384]{3,2,1,0:T(8,128)S(1)}, f32[3,1,16,384]{3,2,1,0:T(8,128)}, u32[]{:S(2)}) copy-start(f32[3,1,16,384]{3,2,1,0:T(8,128)} %param.5) | copy-start | bytes 221188
  1.0 22.5 %collective-permute-start.1 = (f32[3,16,192]{2,1,0:T(8,128)S(1)}, f32[3,16,192]{2,1,0:T(8,128)S(1)}, u32[]{:S(2)}, u32[]{:S(2)}) collective-permute-start(f32[3,16,192]{2,1,0:T(8,128)S(1)} %get-tuple-element.12), channel_id=1, source_target_pairs={{1,0},{2,1},{3,2},{4,3},{5,4},{6,5},{7,6},{8,7},{9,8},{10,9},{11,1... | collective-permute-start | bytes 110600 | tf_op jit(solution)/shard_map/ppermute | solution.py:69
  18.8 15.8 %collective-permute-start = (f32[3,16,192]{2,1,0:T(8,128)S(1)}, f32[3,16,192]{2,1,0:T(8,128)S(1)}, u32[]{:S(2)}, u32[]{:S(2)}) collective-permute-start(f32[3,16,192]{2,1,0:T(8,128)S(1)} %get-tuple-element.11), channel_id=1, source_target_pairs={{0,1},{1,2},{2,3},{3,4},{4,5},{5,6},{6,7},{7,8},{8,9},{9,10},{10,1... | collective-permute-start | bytes 110600 | tf_op jit(solution)/shard_map/ppermute | solution.py:68
  21.5 0.7 %copy-start.5 = (s32[16]{0:T(128)S(1)}, s32[16]{0:T(128)}, u32[]{:S(2)}) copy-start(s32[16]{0:T(128)} %param.6) | copy-start | bytes 196
  22.1 0.7 %copy-start.4 = (f32[4,16]{1,0:T(4,128)S(1)}, f32[4,16]{1,0:T(4,128)}, u32[]{:S(2)}) copy-start(f32[4,16]{1,0:T(4,128)} %param.7) | copy-start | bytes 772
  37.6 5.6 %collective-permute-start.2 = (f32[3,8,384]{2,1,0:T(8,128)}, f32[3,8,384]{2,1,0:T(8,128)S(1)}, u32[]{:S(2)}, u32[]{:S(2)}) collective-permute-start(f32[3,8,384]{2,1,0:T(8,128)} %get-tuple-element.8), channel_id=1, source_target_pairs={{0,16},{16,32},{32,48},{48,64},{64,80},{80,96},{96,112},{112,128},... | collective-permute-start | bytes 110600 | tf_op jit(solution)/shard_map/ppermute | solution.py:81
  40.5 7.6 %collective-permute-start.3 = (f32[3,8,384]{2,1,0:T(8,128)}, f32[3,8,384]{2,1,0:T(8,128)S(1)}, u32[]{:S(2)}, u32[]{:S(2)}) collective-permute-start(f32[3,8,384]{2,1,0:T(8,128)} %get-tuple-element.10), channel_id=1, source_target_pairs={{16,0},{32,16},{48,32},{64,48},{80,64},{96,80},{112,96},{128,112},... | collective-permute-start | bytes 110600 | tf_op jit(solution)/shard_map/ppermute | solution.py:82
  43.2 4.9 %copy-start.2 = (f32[3,8,384]{2,1,0:T(8,128)}, f32[3,8,384]{2,1,0:T(8,128)S(1)}, u32[]{:S(2)}) copy-start(f32[3,8,384]{2,1,0:T(8,128)S(1)} %collective-permute-done.2.up_ref) | copy-start | bytes 110596
  48.1 0.6 %copy-start.3 = (f32[3,8,384]{2,1,0:T(8,128)}, f32[3,8,384]{2,1,0:T(8,128)S(1)}, u32[]{:S(2)}) copy-start(f32[3,8,384]{2,1,0:T(8,128)S(1)} %collective-permute-done.3.down_ref) | copy-start | bytes 110596

commit v4 on v1

v4 whole, which is shorter than its diff:
```python
import jax
import jax.numpy as jnp
from jax import lax
from jax.experimental import pallas as pl
from jax.experimental.pallas import tpu as pltpu
from jax.sharding import PartitionSpec as P

LON_HALO = 256
LAT_HALO = 8
SHIFT_BITS = 9
INTERPRET = False


def row_columns(rows, values):
    row_id = lax.broadcasted_iota(jnp.int32, (rows, 1), 0)
    cols = None
    for j in range(rows):
        here = values(j)
        if cols is None:
            cols = [jnp.full((rows, 1), v, v.dtype) for v in here]
        else:
            cols = [jnp.where(row_id == j, v, c) for v, c in zip(here, cols)]
    return cols


def rotate_rows(row, amount, bits, left):
    width = row.shape[1]
    for b in range(bits):
        step = (width - (1 << b)) if left else (1 << b)
        row = jnp.where(((amount >> b) & 1) == 1, pltpu.roll(row, step, 1), row)
    return row


def pack_kernel(mid_ref, offs_ref, out_ref):
    tracers, rows, width = mid_ref.shape
    need = row_columns(rows, lambda j: [jnp.clip(offs_ref[j] + 1, 0, LON_HALO)])[0]
    for t in range(tracers):
        block = mid_ref[t]
        window = jnp.concatenate(
            [block[:, width - LON_HALO:], block[:, :LON_HALO]], axis=1
        )
        out_ref[t] = rotate_rows(window, LON_HALO - need, SHIFT_BITS, True)[:, :LON_HALO]


def lon_kernel(p_ref, mid_ref, q_ref, par_ref, offs_ref, lw_ref, out_ref, top_ref, bot_ref):
    tracers, rows, width = mid_ref.shape
    ext_width = width + 2 * LON_HALO
    even_lon = par_ref[...] == 0
    cols = row_columns(
        rows,
        lambda j: [LON_HALO - offs_ref[j] - 1, jnp.clip(offs_ref[j] + 1, 0, LON_HALO)]
        + [lw_ref[k, j] for k in range(4)],
    )
    base, need, w = cols[0], cols[1], cols[2:]
    halo_bits = LON_HALO.bit_length() - 1
    masks = [((base >> b) & 1) == 1 for b in range(SHIFT_BITS)]
    for t in range(tracers):
        p, q = p_ref[t], q_ref[t]
        left = rotate_rows(jnp.where(even_lon, q, p), (LON_HALO - need) % LON_HALO, halo_bits, False)
        right = rotate_rows(jnp.where(even_lon, p, q), need, halo_bits, True)
        row = jnp.concatenate([left, mid_ref[t], right], axis=1)
        for b in range(SHIFT_BITS):
            rolled = pltpu.roll(row, ext_width - (1 << b), 1)
            row = jnp.where(masks[b], rolled, row)
        total = jnp.zeros((rows, width), jnp.float32)
        for k in range(4):
            tap = row if k == 0 else pltpu.roll(row, ext_width - k, 1)
            total = total + w[k] * tap[:, :width]
        out_ref[t] = total
        top_ref[t] = total[:LAT_HALO]
        bot_ref[t] = total[rows - LAT_HALO:]


def lat_kernel(up_ref, mid_ref, down_ref, first_ref, offs_ref, lw_ref, out_ref):
    tracers, rows, width = mid_ref.shape
    ext_rows = rows + 2 * LAT_HALO
    nlat = offs_ref.shape[0]
    first = first_ref[0]

    def values(j):
        row = first + j
        shift = offs_ref[row]
        picks = [jnp.clip(row - shift - 1 + k, 0, nlat - 1) - first + LAT_HALO - j for k in range(4)]
        return picks + [lw_ref[k, row] for k in range(4)]

    cols = row_columns(rows, values)
    d, w = cols[:4], cols[4:]
    for t in range(tracers):
        ext = jnp.concatenate([up_ref[t], mid_ref[t], down_ref[t]], axis=0)
        picks = [jnp.zeros((rows, width), jnp.float32) for _ in range(4)]
        for s in range(ext_rows - rows + 1):
            shifted = (ext if s == 0 else pltpu.roll(ext, ext_rows - s, 0))[:rows]
            for k in range(4):
                picks[k] = jnp.where(d[k] == s, shifted, picks[k])
        total = jnp.zeros((rows, width), jnp.float32)
        for k in range(4):
            total = total + w[k] * picks[k]
        out_ref[t] = total


def call(kernel, out_shape, spaces):
    return pl.pallas_call(
        kernel,
        out_shape=out_shape,
        in_specs=[pl.BlockSpec(memory_space=m) for m in spaces],
        interpret=INTERPRET,
    )


def per_device(tracers, lon_offsets, lon_weights, lat_offsets, lat_weights):
    nt, nl, rows, width = tracers.shape
    block = tracers.reshape(nt * nl, rows, width)
    f32 = jnp.float32

    lon_count = lax.axis_size("lon")
    f32 = jnp.float32
    offs = lon_offsets.astype(jnp.int32)
    vmem, smem = pltpu.VMEM, pltpu.SMEM
    packed_shape = jax.ShapeDtypeStruct((nt * nl, rows, LON_HALO), f32)
    packed = call(pack_kernel, packed_shape, [vmem, smem])(block, offs)
    partner = lax.ppermute(packed, "lon", [(i, i ^ 1) for i in range(lon_count)])
    onward = [(i, (i + 2) % lon_count if i % 2 == 0 else (i - 2) % lon_count) for i in range(lon_count)]
    relayed = lax.ppermute(partner, "lon", onward)
    par = (lax.axis_index("lon") % 2).astype(jnp.int32).reshape(1, 1)

    shape = jax.ShapeDtypeStruct((nt * nl, rows, width), f32)
    halo = jax.ShapeDtypeStruct((nt * nl, LAT_HALO, width), f32)
    swept, top, bot = call(lon_kernel, (shape, halo, halo), [vmem] * 4 + [smem] * 2)(
        partner, block, relayed, par, offs, lon_weights.astype(f32)
    )

    lat_count = lax.axis_size("lat")
    down_pairs = [(i, i + 1) for i in range(lat_count - 1)]
    up_pairs = [(i + 1, i) for i in range(lat_count - 1)]
    up = lax.ppermute(bot, "lat", down_pairs)
    down = lax.ppermute(top, "lat", up_pairs)

    first = (lax.axis_index("lat") * rows).astype(jnp.int32).reshape(1)
    out = call(lat_kernel, shape, [vmem] * 3 + [smem] * 3)(
        up, swept, down, first, lat_offsets.astype(jnp.int32), lat_weights.astype(f32)
    )
    return out.reshape(tracers.shape)


def solution(mesh):
    return jax.shard_map(
        per_device,
        mesh=mesh,
        in_specs=(P(None, None, "lat", "lon"), P("lat"), P(None, "lat"), P(), P()),
        out_specs=P(None, None, "lat", "lon"),
        check_vma=False,
    )
```

time: 45.8 us -> 45.5 us (level)
  the two profiles are of different devices: /device:TPU:223 before, /device:TPU:199 now
where the time goes in v4:
time: 45.5 us; the launch traced here: 45.1 us
  starting transfers between devices  24.9 us (55%)
  waiting for transfers between devices  11.9 us (26%)
  Pallas kernels  7.03 us (15%)
  local copies, waits for them, and re-layouts  1.23 us (3%)
    ppermute x1, starting transfers between devices, per_device(): lax.ppermute(packed, 'lon', [(i, i ^ 1) for i in range(lon_count)])  12.1 us
    ppermute x1, starting transfers between devices, per_device(): up = lax.ppermute(bot, 'lat', down_pairs)  7.67 us
    ppermute x1, waiting for transfers between devices, per_device(): down = lax.ppermute(top, 'lat', up_pairs)  6.85 us
    ppermute x1, waiting for transfers between devices, per_device(): relayed = lax.ppermute(partner, 'lon', onward)  3.35 us
    ppermute x1, starting transfers between devices, per_device(): relayed = lax.ppermute(partner, 'lon', onward)  3.19 us
    pallas_call x1, Pallas kernels, per_device(): call(lon_kernel, (shape, halo, halo), [vmem] * 4 + [smem] * 2)  2.79 us
    pallas_call x1, Pallas kernels, per_device(): call(lat_kernel, shape, [vmem] * 3 + [smem] * 3)  2.2 us
    pallas_call x1, Pallas kernels, per_device(): packed = call(pack_kernel, packed_shape, [vmem, smem])(block, offs)  2.04 us
  transfers between devices with their start and end apart: 4, of which 3 were waited for; matrix products, arithmetic and copies ran while one was open for 0% of the time, Pallas kernels for 0%

profile of v4, /device:TPU:199, one launch (start us, length us, event | category | flops | bytes accessed | tf_op | source)
XLA Modules:
  0.0 45.1 jit_solution(17119307551832123769)
XLA Ops:
  0.0 2.0 %shard_map.55 = f32[3,16,256]{2,1,0:T(8,128)} custom-call(f32[3,16,384]{2,1,0:T(8,128)} %bitcast.6, s32[16]{0:T(128)} %offs_ref.4), custom_call_target="tpu_custom_call" | custom-call | tf_op jit(solution)/shard_map/pallas_call | solution.py:120
  2.0 12.1 %collective-permute-start = (f32[3,16,256]{2,1,0:T(8,128)}, f32[3,16,256]{2,1,0:T(8,128)S(1)}, u32[]{:S(2)}, u32[]{:S(2)}) collective-permute-start(f32[3,16,256]{2,1,0:T(8,128)} %shard_map.55), channel_id=1, source_target_pairs={{0,1},{1,0},{2,3},{3,2},{4,5},{5,4},{6,7},{7,6},{8,9},{9,8},{10,11... | collective-permute-start | bytes 147464 | tf_op jit(solution)/shard_map/ppermute | solution.py:121
  14.2 1.7 %collective-permute-done.p_ref = f32[3,16,256]{2,1,0:T(8,128)S(1)} collective-permute-done((f32[3,16,256]{2,1,0:T(8,128)}, f32[3,16,256]{2,1,0:T(8,128)S(1)}, u32[]{:S(2)}, u32[]{:S(2)}) %collective-permute-start) | collective-permute-done | bytes 49184 | tf_op jit(solution)/shard_map/ppermute | solution.py:121
  15.9 0.0 copy-start
  15.9 3.2 %collective-permute-start.1 = (f32[3,16,256]{2,1,0:T(8,128)S(1)}, f32[3,16,256]{2,1,0:T(8,128)S(1)}, u32[]{:S(2)}, u32[]{:S(2)}) collective-permute-start(f32[3,16,256]{2,1,0:T(8,128)S(1)} %collective-permute-done.p_ref), channel_id=1, source_target_pairs={{0,2},{1,15},{2,4},{3,1},{4,6},{5,3},{6,8},{7,5},{8,10},{9,7},{10,... | collective-permute-start | bytes 147464 | tf_op jit(solution)/shard_map/ppermute | solution.py:123
  19.1 3.3 %collective-permute-done.1.q_ref = f32[3,16,256]{2,1,0:T(8,128)S(1)} collective-permute-done((f32[3,16,256]{2,1,0:T(8,128)S(1)}, f32[3,16,256]{2,1,0:T(8,128)S(1)}, u32[]{:S(2)}, u32[]{:S(2)}) %collective-permute-start.1) | collective-permute-done | bytes 49184 | tf_op jit(solution)/shard_map/ppermute | solution.py:123
  22.4 0.0 copy-start.1
  22.4 0.0 copy-done
  22.4 0.6 %copy-done.1 = f32[3,16,256]{2,1,0:T(8,128)} copy-done((f32[3,16,256]{2,1,0:T(8,128)}, f32[3,16,256]{2,1,0:T(8,128)S(1)}, u32[]{:S(2)}) %copy-start.1) | copy-done | bytes 49176
  23.1 2.8 %shard_map.56 = (f32[3,16,384]{2,1,0:T(8,128)}, f32[3,8,384]{2,1,0:T(8,128)}, f32[3,8,384]{2,1,0:T(8,128)}) custom-call(f32[3,16,256]{2,1,0:T(8,128)} %copy-done, f32[3,16,384]{2,1,0:T(8,128)} %bitcast.7, f32[3,16,256]{2,1,0:T(8,128)} %copy-done.1, s32[1,1]{1,0:T(1,128)} %bitcast.1.par_ref, s32[16]{0:T(128)} %offs_ref.4, f32[4,16]{1,0:T(4,128)} %lw_ref.2), custom_call_target="tpu_custom_call" | custom-call | tf_op jit(solution)/shard_map/pallas_call | solution.py:128
  25.8 7.7 %collective-permute-start.2 = (f32[3,8,384]{2,1,0:T(8,128)}, f32[3,8,384]{2,1,0:T(8,128)S(1)}, u32[]{:S(2)}, u32[]{:S(2)}) collective-permute-start(f32[3,8,384]{2,1,0:T(8,128)} %get-tuple-element.8), channel_id=1, source_target_pairs={{0,16},{16,32},{32,48},{48,64},{64,80},{80,96},{96,112},{112,128},... | collective-permute-start | bytes 110600 | tf_op jit(solution)/shard_map/ppermute | solution.py:135
  33.5 1.9 %collective-permute-start.3 = (f32[3,8,384]{2,1,0:T(8,128)}, f32[3,8,384]{2,1,0:T(8,128)S(1)}, u32[]{:S(2)}, u32[]{:S(2)}) collective-permute-start(f32[3,8,384]{2,1,0:T(8,128)} %get-tuple-element.10), channel_id=1, source_target_pairs={{16,0},{32,16},{48,32},{64,48},{80,64},{96,80},{112,96},{128,112},... | collective-permute-start | bytes 110600 | tf_op jit(solution)/shard_map/ppermute | solution.py:136
  35.5 0.0 collective-permute-done.2.up_ref
  35.5 0.0 copy-start.2
  35.5 6.8 %collective-permute-done.3.down_ref = f32[3,8,384]{2,1,0:T(8,128)S(1)} collective-permute-done((f32[3,8,384]{2,1,0:T(8,128)}, f32[3,8,384]{2,1,0:T(8,128)S(1)}, u32[]{:S(2)}, u32[]{:S(2)}) %collective-permute-start.3) | collective-permute-done | bytes 36896 | tf_op jit(solution)/shard_map/ppermute | solution.py:136
  42.3 0.0 copy-start.3
  42.3 0.0 copy-done.2
  42.3 0.6 %copy-done.3 = f32[3,8,384]{2,1,0:T(8,128)} copy-done((f32[3,8,384]{2,1,0:T(8,128)}, f32[3,8,384]{2,1,0:T(8,128)S(1)}, u32[]{:S(2)}) %copy-start.3) | copy-done | bytes 36888
  42.9 2.2 %shard_map.57 = f32[3,16,384]{2,1,0:T(8,128)} custom-call(f32[3,8,384]{2,1,0:T(8,128)} %copy-done.2, f32[3,16,384]{2,1,0:T(8,128)} %get-tuple-element.9.mid_ref, f32[3,8,384]{2,1,0:T(8,128)} %copy-done.3, s32[1]{0:T(128)} %bitcast.2.first_ref, s32[768]{0:T(1024)} %offs_ref.5, f32[4,768]{1,0:T(4,128)} %lw_ref.3), custom_call_target="tpu_custom_call" | custom-call | tf_op jit(solution)/shard_map/pallas_call | solution.py:139
Async XLA Ops:
  2.0 13.8 %collective-permute-start = (f32[3,16,256]{2,1,0:T(8,128)}, f32[3,16,256]{2,1,0:T(8,128)S(1)}, u32[]{:S(2)}, u32[]{:S(2)}) collective-permute-start(f32[3,16,256]{2,1,0:T(8,128)} %shard_map.55), channel_id=1, source_target_pairs={{0,1},{1,0},{2,3},{3,2},{4,5},{5,4},{6,7},{7,6},{8,9},{9,8},{10,11... | collective-permute-start | bytes 147464 | tf_op jit(solution)/shard_map/ppermute | solution.py:121
  15.9 6.6 %copy-start = (f32[3,16,256]{2,1,0:T(8,128)}, f32[3,16,256]{2,1,0:T(8,128)S(1)}, u32[]{:S(2)}) copy-start(f32[3,16,256]{2,1,0:T(8,128)S(1)} %collective-permute-done.p_ref) | copy-start | bytes 147460
  15.9 6.6 %collective-permute-start.1 = (f32[3,16,256]{2,1,0:T(8,128)S(1)}, f32[3,16,256]{2,1,0:T(8,128)S(1)}, u32[]{:S(2)}, u32[]{:S(2)}) collective-permute-start(f32[3,16,256]{2,1,0:T(8,128)S(1)} %collective-permute-done.p_ref), channel_id=1, source_target_pairs={{0,2},{1,15},{2,4},{3,1},{4,6},{5,3},{6,8},{7,5},{8,10},{9,7},{10,... | collective-permute-start | bytes 147464 | tf_op jit(solution)/shard_map/ppermute | solution.py:123
  22.4 0.6 %copy-start.1 = (f32[3,16,256]{2,1,0:T(8,128)}, f32[3,16,256]{2,1,0:T(8,128)S(1)}, u32[]{:S(2)}) copy-start(f32[3,16,256]{2,1,0:T(8,128)S(1)} %collective-permute-done.1.q_ref) | copy-start | bytes 147460
  25.8 9.6 %collective-permute-start.2 = (f32[3,8,384]{2,1,0:T(8,128)}, f32[3,8,384]{2,1,0:T(8,128)S(1)}, u32[]{:S(2)}, u32[]{:S(2)}) collective-permute-start(f32[3,8,384]{2,1,0:T(8,128)} %get-tuple-element.8), channel_id=1, source_target_pairs={{0,16},{16,32},{32,48},{48,64},{64,80},{80,96},{96,112},{112,128},... | collective-permute-start | bytes 110600 | tf_op jit(solution)/shard_map/ppermute | solution.py:135
  33.5 8.8 %collective-permute-start.3 = (f32[3,8,384]{2,1,0:T(8,128)}, f32[3,8,384]{2,1,0:T(8,128)S(1)}, u32[]{:S(2)}, u32[]{:S(2)}) collective-permute-start(f32[3,8,384]{2,1,0:T(8,128)} %get-tuple-element.10), channel_id=1, source_target_pairs={{16,0},{32,16},{48,32},{64,48},{80,64},{96,80},{112,96},{128,112},... | collective-permute-start | bytes 110600 | tf_op jit(solution)/shard_map/ppermute | solution.py:136
  35.5 6.9 %copy-start.2 = (f32[3,8,384]{2,1,0:T(8,128)}, f32[3,8,384]{2,1,0:T(8,128)S(1)}, u32[]{:S(2)}) copy-start(f32[3,8,384]{2,1,0:T(8,128)S(1)} %collective-permute-done.2.up_ref) | copy-start | bytes 110596
  42.3 0.6 %copy-start.3 = (f32[3,8,384]{2,1,0:T(8,128)}, f32[3,8,384]{2,1,0:T(8,128)S(1)}, u32[]{:S(2)}) copy-start(f32[3,8,384]{2,1,0:T(8,128)S(1)} %collective-permute-done.3.down_ref) | copy-start | bytes 110596

commit v5 on v4

--- a/solution.py
+++ b/solution.py
@@ -8,6 +8,7 @@
 LON_HALO = 256
 LAT_HALO = 8
 SHIFT_BITS = 9
+PACK_SHIFT = 64
 INTERPRET = False
 
 
@@ -31,17 +32,6 @@
     return row
 
 
-def pack_kernel(mid_ref, offs_ref, out_ref):
-    tracers, rows, width = mid_ref.shape
-    need = row_columns(rows, lambda j: [jnp.clip(offs_ref[j] + 1, 0, LON_HALO)])[0]
-    for t in range(tracers):
-        block = mid_ref[t]
-        window = jnp.concatenate(
-            [block[:, width - LON_HALO:], block[:, :LON_HALO]], axis=1
-        )
-        out_ref[t] = rotate_rows(window, LON_HALO - need, SHIFT_BITS, True)[:, :LON_HALO]
-
-
 def lon_kernel(p_ref, mid_ref, q_ref, par_ref, offs_ref, lw_ref, out_ref, top_ref, bot_ref):
     tracers, rows, width = mid_ref.shape
     ext_width = width + 2 * LON_HALO
@@ -52,12 +42,13 @@
         + [lw_ref[k, j] for k in range(4)],
     )
     base, need, w = cols[0], cols[1], cols[2:]
-    halo_bits = LON_HALO.bit_length() - 1
+    ahead = need > 0
     masks = [((base >> b) & 1) == 1 for b in range(SHIFT_BITS)]
     for t in range(tracers):
         p, q = p_ref[t], q_ref[t]
-        left = rotate_rows(jnp.where(even_lon, q, p), (LON_HALO - need) % LON_HALO, halo_bits, False)
-        right = rotate_rows(jnp.where(even_lon, p, q), need, halo_bits, True)
+        left = pltpu.roll(jnp.where(even_lon, q, p), PACK_SHIFT, 1)
+        right = jnp.where(even_lon, p, q)
+        right = jnp.where(ahead, pltpu.roll(right, PACK_SHIFT, 1), right)
         row = jnp.concatenate([left, mid_ref[t], right], axis=1)
         for b in range(SHIFT_BITS):
             rolled = pltpu.roll(row, ext_width - (1 << b), 1)
@@ -116,8 +107,13 @@
     f32 = jnp.float32
     offs = lon_offsets.astype(jnp.int32)
     vmem, smem = pltpu.VMEM, pltpu.SMEM
-    packed_shape = jax.ShapeDtypeStruct((nt * nl, rows, LON_HALO), f32)
-    packed = call(pack_kernel, packed_shape, [vmem, smem])(block, offs)
+    tail = width - LON_HALO + PACK_SHIFT
+    ahead = (offs >= 0)[None, :, None]
+    packed = jnp.where(
+        ahead,
+        jnp.concatenate([block[:, :, tail:], block[:, :, :LON_HALO - width + tail]], axis=2),
+        block[:, :, :LON_HALO],
+    )
     partner = lax.ppermute(packed, "lon", [(i, i ^ 1) for i in range(lon_count)])
     onward = [(i, (i + 2) % lon_count if i % 2 == 0 else (i - 2) % lon_count) for i in range(lon_count)]
     relayed = lax.ppermute(partner, "lon", onward)

time: 45.5 us -> 44.7 us (0.982)
  Pallas kernels: 7.03 us -> 4.59 us
  local copies, waits for them, and re-layouts: 1.23 us -> 2.95 us
    pallas_call x1 -> x0, Pallas kernels: 2.04 us -> none  [per_device(): packed = call(pack_kernel, packed_shape, [vmem, smem])(block, offs)]
    slice x0 -> x2, local copies, waits for them, and re-layouts: none -> 1.7 us  [the longest x1 0.89 us: per_device(): block[:, :, tail:]]
    unnamed x8 -> x12, local copies, waits for them, and re-layouts: 1.23 us -> 1.25 us
where the time goes in v5:
time: 44.7 us; the launch traced here: 44.3 us
  starting transfers between devices  24.9 us (56%)
  waiting for transfers between devices  11.7 us (26%)
  Pallas kernels  4.59 us (10%)
  local copies, waits for them, and re-layouts  2.95 us (7%)
    ppermute x1, starting transfers between devices, per_device(): lax.ppermute(packed, 'lon', [(i, i ^ 1) for i in range(lon_count)])  12.2 us
    ppermute x1, starting transfers between devices, per_device(): up = lax.ppermute(bot, 'lat', down_pairs)  7.67 us
    ppermute x1, waiting for transfers between devices, per_device(): down = lax.ppermute(top, 'lat', up_pairs)  6.85 us
    ppermute x1, waiting for transfers between devices, per_device(): relayed = lax.ppermute(partner, 'lon', onward)  3.35 us
    ppermute x1, starting transfers between devices, per_device(): relayed = lax.ppermute(partner, 'lon', onward)  3.19 us
    pallas_call x1, Pallas kernels, per_device(): call(lon_kernel, (shape, halo, halo), [vmem] * 4 + [smem] * 2)  2.39 us
    pallas_call x1, Pallas kernels, per_device(): call(lat_kernel, shape, [vmem] * 3 + [smem] * 3)  2.2 us
    ppermute x1, starting transfers between devices, per_device(): down = lax.ppermute(top, 'lat', up_pairs)  1.92 us
  transfers between devices with their start and end apart: 4, of which 3 were waited for; matrix products, arithmetic and copies ran while one was open for 0% of the time, Pallas kernels for 0%

profile of v5, /device:TPU:199, one launch (start us, length us, event | category | flops | bytes accessed | tf_op | source)
XLA Modules:
  0.0 44.3 jit_solution(9871579335423622614)
XLA Ops:
  0.0 0.0 copy-start
  0.0 0.8 %slice.13 = f32[3,16,64]{2,1,0:T(8,128)S(1)} slice(f32[3,16,384]{2,1,0:T(8,128)} %bitcast.6), slice={[0:3], [0:16], [0:64]} | slice | bytes 24576 | tf_op jit(solution)/shard_map/slice | solution.py:114
  0.8 0.0 copy-start.5
  0.8 0.9 %slice.12 = f32[3,16,192]{2,1,0:T(8,128)S(1)} slice(f32[3,16,384]{2,1,0:T(8,128)} %bitcast.7), slice={[0:3], [0:16], [192:384]} | slice | bytes 73728 | tf_op jit(solution)/shard_map/slice | solution.py:114
  1.7 0.0 copy-done.5
  1.7 0.0 copy-done
  1.7 0.1 slice_select_fusion
  1.8 12.2 %collective-permute-start = (f32[3,16,256]{2,1,0:T(8,128)S(1)}, f32[3,16,256]{2,1,0:T(8,128)S(1)}, u32[]{:S(2)}, u32[]{:S(2)}) collective-permute-start(f32[3,16,256]{2,1,0:T(8,128)S(1)} %slice_select_fusion), channel_id=1, source_target_pairs={{0,1},{1,0},{2,3},{3,2},{4,5},{5,4},{6,7},{7,6},{8,9},{9,8},{10,11... | collective-permute-start | bytes 147464 | tf_op jit(solution)/shard_map/ppermute | solution.py:117
  14.0 1.5 %collective-permute-done.p_ref = f32[3,16,256]{2,1,0:T(8,128)S(1)} collective-permute-done((f32[3,16,256]{2,1,0:T(8,128)S(1)}, f32[3,16,256]{2,1,0:T(8,128)S(1)}, u32[]{:S(2)}, u32[]{:S(2)}) %collective-permute-start) | collective-permute-done | bytes 49184 | tf_op jit(solution)/shard_map/ppermute | solution.py:117
  15.4 0.0 copy-start.1
  15.4 3.2 %collective-permute-start.1 = (f32[3,16,256]{2,1,0:T(8,128)S(1)}, f32[3,16,256]{2,1,0:T(8,128)S(1)}, u32[]{:S(2)}, u32[]{:S(2)}) collective-permute-start(f32[3,16,256]{2,1,0:T(8,128)S(1)} %collective-permute-done.p_ref), channel_id=1, source_target_pairs={{0,2},{1,15},{2,4},{3,1},{4,6},{5,3},{6,8},{7,5},{8,10},{9,7},{10,... | collective-permute-start | bytes 147464 | tf_op jit(solution)/shard_map/ppermute | solution.py:119
  18.7 3.3 %collective-permute-done.1.q_ref = f32[3,16,256]{2,1,0:T(8,128)S(1)} collective-permute-done((f32[3,16,256]{2,1,0:T(8,128)S(1)}, f32[3,16,256]{2,1,0:T(8,128)S(1)}, u32[]{:S(2)}, u32[]{:S(2)}) %collective-permute-start.1) | collective-permute-done | bytes 49184 | tf_op jit(solution)/shard_map/ppermute | solution.py:119
  22.0 0.0 copy-start.2
  22.0 0.0 copy-done.1
  22.0 0.6 %copy-done.2 = f32[3,16,256]{2,1,0:T(8,128)} copy-done((f32[3,16,256]{2,1,0:T(8,128)}, f32[3,16,256]{2,1,0:T(8,128)S(1)}, u32[]{:S(2)}) %copy-start.2) | copy-done | bytes 49176
  22.6 2.4 %shard_map.55 = (f32[3,16,384]{2,1,0:T(8,128)}, f32[3,8,384]{2,1,0:T(8,128)}, f32[3,8,384]{2,1,0:T(8,128)}) custom-call(f32[3,16,256]{2,1,0:T(8,128)} %copy-done.1, f32[3,16,384]{2,1,0:T(8,128)} %bitcast.8, f32[3,16,256]{2,1,0:T(8,128)} %copy-done.2, s32[1,1]{1,0:T(1,128)} %bitcast.1.par_ref, s32[16]{0:T(128)} %offs_ref.2, f32[4,16]{1,0:T(4,128)} %lw_ref.2), custom_call_target="tpu_custom_call" | custom-call | tf_op jit(solution)/shard_map/pallas_call | solution.py:124
  25.0 7.7 %collective-permute-start.2 = (f32[3,8,384]{2,1,0:T(8,128)}, f32[3,8,384]{2,1,0:T(8,128)S(1)}, u32[]{:S(2)}, u32[]{:S(2)}) collective-permute-start(f32[3,8,384]{2,1,0:T(8,128)} %get-tuple-element.8), channel_id=1, source_target_pairs={{0,16},{16,32},{32,48},{48,64},{64,80},{80,96},{96,112},{112,128},... | collective-permute-start | bytes 110600 | tf_op jit(solution)/shard_map/ppermute | solution.py:131
  32.7 1.9 %collective-permute-start.3 = (f32[3,8,384]{2,1,0:T(8,128)}, f32[3,8,384]{2,1,0:T(8,128)S(1)}, u32[]{:S(2)}, u32[]{:S(2)}) collective-permute-start(f32[3,8,384]{2,1,0:T(8,128)} %get-tuple-element.10), channel_id=1, source_target_pairs={{16,0},{32,16},{48,32},{64,48},{80,64},{96,80},{112,96},{128,112},... | collective-permute-start | bytes 110600 | tf_op jit(solution)/shard_map/ppermute | solution.py:132
  34.6 0.0 collective-permute-done.2.up_ref
  34.6 0.0 copy-start.3
  34.6 6.8 %collective-permute-done.3.down_ref = f32[3,8,384]{2,1,0:T(8,128)S(1)} collective-permute-done((f32[3,8,384]{2,1,0:T(8,128)}, f32[3,8,384]{2,1,0:T(8,128)S(1)}, u32[]{:S(2)}, u32[]{:S(2)}) %collective-permute-start.3) | collective-permute-done | bytes 36896 | tf_op jit(solution)/shard_map/ppermute | solution.py:132
  41.5 0.0 copy-start.4
  41.5 0.0 copy-done.3
  41.5 0.6 %copy-done.4 = f32[3,8,384]{2,1,0:T(8,128)} copy-done((f32[3,8,384]{2,1,0:T(8,128)}, f32[3,8,384]{2,1,0:T(8,128)S(1)}, u32[]{:S(2)}) %copy-start.4) | copy-done | bytes 36888
  42.1 2.2 %shard_map.56 = f32[3,16,384]{2,1,0:T(8,128)} custom-call(f32[3,8,384]{2,1,0:T(8,128)} %copy-done.3, f32[3,16,384]{2,1,0:T(8,128)} %get-tuple-element.9.mid_ref, f32[3,8,384]{2,1,0:T(8,128)} %copy-done.4, s32[1]{0:T(128)} %bitcast.2.first_ref, s32[768]{0:T(1024)} %offs_ref.3, f32[4,768]{1,0:T(4,128)} %lw_ref.3), custom_call_target="tpu_custom_call" | custom-call | tf_op jit(solution)/shard_map/pallas_call | solution.py:135
  (1 shorter events, 0.0 us)
Async XLA Ops:
  0.0 1.7 %copy-start = (f32[3,1,16,384]{3,2,1,0:T(8,128)S(1)}, f32[3,1,16,384]{3,2,1,0:T(8,128)}, u32[]{:S(2)}) copy-start(f32[3,1,16,384]{3,2,1,0:T(8,128)} %param.5) | copy-start | bytes 221188
  0.8 0.9 %copy-start.5 = (s32[16]{0:T(128)S(1)}, s32[16]{0:T(128)}, u32[]{:S(2)}) copy-start(s32[16]{0:T(128)} %offs_ref.2) | copy-start | bytes 196
  1.8 13.6 %collective-permute-start = (f32[3,16,256]{2,1,0:T(8,128)S(1)}, f32[3,16,256]{2,1,0:T(8,128)S(1)}, u32[]{:S(2)}, u32[]{:S(2)}) collective-permute-start(f32[3,16,256]{2,1,0:T(8,128)S(1)} %slice_select_fusion), channel_id=1, source_target_pairs={{0,1},{1,0},{2,3},{3,2},{4,5},{5,4},{6,7},{7,6},{8,9},{9,8},{10,11... | collective-permute-start | bytes 147464 | tf_op jit(solution)/shard_map/ppermute | solution.py:117
  15.4 6.6 %copy-start.1 = (f32[3,16,256]{2,1,0:T(8,128)}, f32[3,16,256]{2,1,0:T(8,128)S(1)}, u32[]{:S(2)}) copy-start(f32[3,16,256]{2,1,0:T(8,128)S(1)} %collective-permute-done.p_ref) | copy-start | bytes 147460
  15.4 6.6 %collective-permute-start.1 = (f32[3,16,256]{2,1,0:T(8,128)S(1)}, f32[3,16,256]{2,1,0:T(8,128)S(1)}, u32[]{:S(2)}, u32[]{:S(2)}) collective-permute-start(f32[3,16,256]{2,1,0:T(8,128)S(1)} %collective-permute-done.p_ref), channel_id=1, source_target_pairs={{0,2},{1,15},{2,4},{3,1},{4,6},{5,3},{6,8},{7,5},{8,10},{9,7},{10,... | collective-permute-start | bytes 147464 | tf_op jit(solution)/shard_map/ppermute | solution.py:119
  22.0 0.6 %copy-start.2 = (f32[3,16,256]{2,1,0:T(8,128)}, f32[3,16,256]{2,1,0:T(8,128)S(1)}, u32[]{:S(2)}) copy-start(f32[3,16,256]{2,1,0:T(8,128)S(1)} %collective-permute-done.1.q_ref) | copy-start | bytes 147460
  25.0 9.6 %collective-permute-start.2 = (f32[3,8,384]{2,1,0:T(8,128)}, f32[3,8,384]{2,1,0:T(8,128)S(1)}, u32[]{:S(2)}, u32[]{:S(2)}) collective-permute-start(f32[3,8,384]{2,1,0:T(8,128)} %get-tuple-element.8), channel_id=1, source_target_pairs={{0,16},{16,32},{32,48},{48,64},{64,80},{80,96},{96,112},{112,128},... | collective-permute-start | bytes 110600 | tf_op jit(solution)/shard_map/ppermute | solution.py:131
  32.7 8.8 %collective-permute-start.3 = (f32[3,8,384]{2,1,0:T(8,128)}, f32[3,8,384]{2,1,0:T(8,128)S(1)}, u32[]{:S(2)}, u32[]{:S(2)}) collective-permute-start(f32[3,8,384]{2,1,0:T(8,128)} %get-tuple-element.10), channel_id=1, source_target_pairs={{16,0},{32,16},{48,32},{64,48},{80,64},{96,80},{112,96},{128,112},... | collective-permute-start | bytes 110600 | tf_op jit(solution)/shard_map/ppermute | solution.py:132
  34.6 6.9 %copy-start.3 = (f32[3,8,384]{2,1,0:T(8,128)}, f32[3,8,384]{2,1,0:T(8,128)S(1)}, u32[]{:S(2)}) copy-start(f32[3,8,384]{2,1,0:T(8,128)S(1)} %collective-permute-done.2.up_ref) | copy-start | bytes 110596
  41.5 0.6 %copy-start.4 = (f32[3,8,384]{2,1,0:T(8,128)}, f32[3,8,384]{2,1,0:T(8,128)S(1)}, u32[]{:S(2)}) copy-start(f32[3,8,384]{2,1,0:T(8,128)S(1)} %collective-permute-done.3.down_ref) | copy-start | bytes 110596

commit v6 on v5

--- a/solution.py
+++ b/solution.py
@@ -36,13 +36,9 @@
     tracers, rows, width = mid_ref.shape
     ext_width = width + 2 * LON_HALO
     even_lon = par_ref[...] == 0
-    cols = row_columns(
-        rows,
-        lambda j: [LON_HALO - offs_ref[j] - 1, jnp.clip(offs_ref[j] + 1, 0, LON_HALO)]
-        + [lw_ref[k, j] for k in range(4)],
-    )
-    base, need, w = cols[0], cols[1], cols[2:]
-    ahead = need > 0
+    base = offs_ref[...]
+    w = [lw_ref[:, k:k + 1] for k in range(4)]
+    ahead = base < LON_HALO
     masks = [((base >> b) & 1) == 1 for b in range(SHIFT_BITS)]
     for t in range(tracers):
         p, q = p_ref[t], q_ref[t]
@@ -62,25 +58,16 @@
         bot_ref[t] = total[rows - LAT_HALO:]
 
 
-def lat_kernel(up_ref, mid_ref, down_ref, first_ref, offs_ref, lw_ref, out_ref):
+def lat_kernel(up_ref, mid_ref, down_ref, offs_ref, lw_ref, out_ref):
     tracers, rows, width = mid_ref.shape
     ext_rows = rows + 2 * LAT_HALO
-    nlat = offs_ref.shape[0]
-    first = first_ref[0]
-
-    def values(j):
-        row = first + j
-        shift = offs_ref[row]
-        picks = [jnp.clip(row - shift - 1 + k, 0, nlat - 1) - first + LAT_HALO - j for k in range(4)]
-        return picks + [lw_ref[k, row] for k in range(4)]
-
-    cols = row_columns(rows, values)
-    d, w = cols[:4], cols[4:]
+    d = [offs_ref[:, k:k + 1] for k in range(4)]
+    w = [lw_ref[:, k:k + 1] for k in range(4)]
     for t in range(tracers):
         ext = jnp.concatenate([up_ref[t], mid_ref[t], down_ref[t]], axis=0)
         picks = [jnp.zeros((rows, width), jnp.float32) for _ in range(4)]
-        for s in range(ext_rows - rows + 1):
-            shifted = (ext if s == 0 else pltpu.roll(ext, ext_rows - s, 0))[:rows]
+        for s in range(LAT_HALO - 5, LAT_HALO + 7):
+            shifted = pltpu.roll(ext, ext_rows - s, 0)[:rows]
             for k in range(4):
                 picks[k] = jnp.where(d[k] == s, shifted, picks[k])
         total = jnp.zeros((rows, width), jnp.float32)
@@ -121,8 +108,10 @@
 
     shape = jax.ShapeDtypeStruct((nt * nl, rows, width), f32)
     halo = jax.ShapeDtypeStruct((nt * nl, LAT_HALO, width), f32)
-    swept, top, bot = call(lon_kernel, (shape, halo, halo), [vmem] * 4 + [smem] * 2)(
-        partner, block, relayed, par, offs, lon_weights.astype(f32)
+    base = (LON_HALO - offs - 1).reshape(rows, 1)
+    lw = jnp.transpose(lon_weights).astype(f32)
+    swept, top, bot = call(lon_kernel, (shape, halo, halo), [vmem] * 6)(
+        partner, block, relayed, par, base, lw
     )
 
     lat_count = lax.axis_size("lat")
@@ -131,9 +120,16 @@
     up = lax.ppermute(bot, "lat", down_pairs)
     down = lax.ppermute(top, "lat", up_pairs)
 
-    first = (lax.axis_index("lat") * rows).astype(jnp.int32).reshape(1)
-    out = call(lat_kernel, shape, [vmem] * 3 + [smem] * 3)(
-        up, swept, down, first, lat_offsets.astype(jnp.int32), lat_weights.astype(f32)
+    nlat = lat_offsets.shape[0]
+    first = lax.axis_index("lat") * rows
+    own = first + jnp.arange(rows, dtype=jnp.int32)
+    lat_offs = lax.dynamic_slice_in_dim(lat_offsets, first, rows)
+    lat_w = lax.dynamic_slice_in_dim(lat_weights, first, rows, axis=1)
+    taps = jnp.arange(4, dtype=jnp.int32)
+    source = jnp.clip(own[:, None] - lat_offs[:, None] - 1 + taps[None, :], 0, nlat - 1)
+    d = (source - first + LAT_HALO - jnp.arange(rows, dtype=jnp.int32)[:, None]).astype(jnp.int32)
+    out = call(lat_kernel, shape, [vmem] * 5)(
+        up, swept, down, d, jnp.transpose(lat_w).astype(f32)
     )
     return out.reshape(tracers.shape)
 

time: 44.7 us -> 44.2 us (0.989)
  waiting for transfers between devices: 11.7 us -> 8.09 us
  local copies, waits for them, and re-layouts: 2.95 us -> 4.93 us
  other arithmetic: 0.09 us -> 1.53 us
    unnamed x12 -> x18, local copies, waits for them, and re-layouts: 1.25 us -> 3.23 us
    ppermute x1, waiting for transfers between devices: 1.46 us -> 0.01 us  [per_device(): lax.ppermute(packed, 'lon', [(i, i ^ 1) for i in range(lon_count)])]
    sub x0 -> x2, other arithmetic: none -> 1.44 us  [the longest x1 0.77 us: per_device(): own[:, None] - lat_offs[:, None] - 1 + taps[None, :]]
    ppermute x1, waiting for transfers between devices: 3.35 us -> 1.98 us  [per_device(): relayed = lax.ppermute(partner, 'lon', onward)]
    slice x1, local copies, waits for them, and re-layouts: 0.81 us -> 0.01 us  [per_device(): block[:, :, :LON_HALO - width + tail]]
    ppermute x1, waiting for transfers between devices: 6.85 us -> 6.11 us  [per_device(): down = lax.ppermute(top, 'lat', up_pairs)]
    reshape x0 -> x1, local copies, waits for them, and re-layouts: none -> 0.67 us  [per_device(): base = (LON_HALO - offs - 1).reshape(rows, 1)]
  transfers between devices with their start and end apart: 4 -> 4, of which waited for: 3 -> 2; matrix products, arithmetic and copies ran while one was open for 0% -> 8% of each run, Pallas kernels for 0% -> 0%
where the time goes in v6:
time: 44.2 us; the launch traced here: 43.8 us
  starting transfers between devices  24.9 us (56%)
  waiting for transfers between devices  8.09 us (18%)
  local copies, waits for them, and re-layouts  4.93 us (11%)
  Pallas kernels  4.18 us (9%)
  other arithmetic  1.53 us (3%)
    ppermute x1, starting transfers between devices, per_device(): lax.ppermute(packed, 'lon', [(i, i ^ 1) for i in range(lon_count)])  12.2 us
    ppermute x1, starting transfers between devices, per_device(): up = lax.ppermute(bot, 'lat', down_pairs)  7.67 us
    ppermute x1, waiting for transfers between devices, per_device(): down = lax.ppermute(top, 'lat', up_pairs)  6.11 us
    unnamed x18, local copies, waits for them, and re-layouts  3.23 us
    ppermute x1, starting transfers between devices, per_device(): relayed = lax.ppermute(partner, 'lon', onward)  3.19 us
    pallas_call x1, Pallas kernels, per_device(): call(lon_kernel, (shape, halo, halo), [vmem] * 6)  2.37 us
    ppermute x1, waiting for transfers between devices, per_device(): relayed = lax.ppermute(partner, 'lon', onward)  1.98 us
    ppermute x1, starting transfers between devices, per_device(): down = lax.ppermute(top, 'lat', up_pairs)  1.92 us
  transfers between devices with their start and end apart: 4, of which 2 were waited for; matrix products, arithmetic and copies ran while one was open for 8% of the time, Pallas kernels for 0%

profile of v6, /device:TPU:199, one launch (start us, length us, event | category | flops | bytes accessed | tf_op | source)
XLA Modules:
  0.0 43.8 jit_solution(4900383047364464188)
XLA Ops:
  0.0 0.0 copy-start
  0.0 0.0 copy-start.1
  0.0 0.9 %slice.12 = f32[3,16,192]{2,1,0:T(8,128)S(1)} slice(f32[3,16,384]{2,1,0:T(8,128)} %bitcast.9), slice={[0:3], [0:16], [192:384]} | slice | bytes 73728 | tf_op jit(solution)/shard_map/slice | solution.py:101
  0.9 0.0 copy-done.1
  1.0 0.0 copy-start.7
  1.0 0.6 %copy-done.7 = s32[16]{0:T(128)S(1)} copy-done((s32[16]{0:T(128)S(1)}, s32[16]{0:T(128)}, u32[]{:S(2)}) %copy-start.7) | copy-done | bytes 88
  1.6 0.1 slice_select_fusion
  1.7 12.2 %collective-permute-start = (f32[3,16,256]{2,1,0:T(8,128)S(1)}, f32[3,16,256]{2,1,0:T(8,128)S(1)}, u32[]{:S(2)}, u32[]{:S(2)}) collective-permute-start(f32[3,16,256]{2,1,0:T(8,128)S(1)} %slice_select_fusion), channel_id=1, source_target_pairs={{0,1},{1,0},{2,3},{3,2},{4,5},{5,4},{6,7},{7,6},{8,9},{9,8},{10,11... | collective-permute-start | bytes 147464 | tf_op jit(solution)/shard_map/ppermute | solution.py:104
  13.9 0.8 %subtract_add_fusion = s32[16]{0:T(128)S(1)} fusion(s32[768]{0:T(1024)} %param.8, s32[]{:T(128)S(6)} %select_n.17, s32[]{:T(128)S(6)} %mul.3), kind=kLoop, calls=%fused_computation.2 | loop fusion | flops 48 | bytes 136 | tf_op jit(solution)/shard_map/sub | solution.py:129
  14.6 0.7 %iota_subtract_fusion.offs_ref = s32[16,4]{1,0:T(8,128)} fusion(s32[]{:T(128)S(6)} %mul.3, s32[16]{0:T(128)S(1)} %subtract_add_fusion), kind=kLoop, calls=%fused_computation.1 | loop fusion | flops 320 | bytes 324 | tf_op jit(solution)/shard_map/sub | solution.py:130
  15.3 0.0 collective-permute-done.p_ref
  15.3 0.0 copy-start.2
  15.3 3.2 %collective-permute-start.1 = (f32[3,16,256]{2,1,0:T(8,128)S(1)}, f32[3,16,256]{2,1,0:T(8,128)S(1)}, u32[]{:S(2)}, u32[]{:S(2)}) collective-permute-start(f32[3,16,256]{2,1,0:T(8,128)S(1)} %collective-permute-done.p_ref), channel_id=1, source_target_pairs={{0,2},{1,15},{2,4},{3,1},{4,6},{5,3},{6,8},{7,5},{8,10},{9,7},{10,... | collective-permute-start | bytes 147464 | tf_op jit(solution)/shard_map/ppermute | solution.py:106
  18.6 0.0 copy-start.6
  18.6 0.7 %copy.7.offs_ref = s32[16,1]{1,0:T(8,128)} copy(s32[16,1]{0,1:T(1,128)S(1)} %subtract_bitcast_fusion) | data formatting | bytes 128 | tf_op jit(solution)/shard_map/reshape | solution.py:111
  19.2 0.0 copy-done.6
  19.2 0.7 %copy.6 = f32[4,16]{0,1:T(8,128)} copy(f32[4,16]{1,0:T(4,128)S(1)} %copy-done.6) | data formatting | bytes 512 | tf_op args[2]
  19.9 2.0 %collective-permute-done.1.q_ref = f32[3,16,256]{2,1,0:T(8,128)S(1)} collective-permute-done((f32[3,16,256]{2,1,0:T(8,128)S(1)}, f32[3,16,256]{2,1,0:T(8,128)S(1)}, u32[]{:S(2)}, u32[]{:S(2)}) %collective-permute-start.1) | collective-permute-done | bytes 49184 | tf_op jit(solution)/shard_map/ppermute | solution.py:106
  21.9 0.0 copy-start.3
  21.9 0.0 copy-done.2
  21.9 0.6 %copy-done.3 = f32[3,16,256]{2,1,0:T(8,128)} copy-done((f32[3,16,256]{2,1,0:T(8,128)}, f32[3,16,256]{2,1,0:T(8,128)S(1)}, u32[]{:S(2)}) %copy-start.3) | copy-done | bytes 49176
  22.5 2.4 %shard_map.55 = (f32[3,16,384]{2,1,0:T(8,128)}, f32[3,8,384]{2,1,0:T(8,128)}, f32[3,8,384]{2,1,0:T(8,128)}) custom-call(f32[3,16,256]{2,1,0:T(8,128)} %copy-done.2, f32[3,16,384]{2,1,0:T(8,128)} %bitcast.10, f32[3,16,256]{2,1,0:T(8,128)} %copy-done.3, s32[1,1]{1,0:T(1,128)} %bitcast.1.par_ref, s32[16,1]{1,0:T(8,128)} %copy.7.offs_ref, f32[16,4]{1,0:T(8,128)} %bitcast.13), custom_call_target="tpu_custom_call" | custom-call | tf_op jit(solution)/shard_map/pallas_call | solution.py:113
  24.9 7.7 %collective-permute-start.2 = (f32[3,8,384]{2,1,0:T(8,128)}, f32[3,8,384]{2,1,0:T(8,128)S(1)}, u32[]{:S(2)}, u32[]{:S(2)}) collective-permute-start(f32[3,8,384]{2,1,0:T(8,128)} %get-tuple-element.8), channel_id=1, source_target_pairs={{0,16},{16,32},{32,48},{48,64},{64,80},{80,96},{96,112},{112,128},... | collective-permute-start | bytes 110600 | tf_op jit(solution)/shard_map/ppermute | solution.py:120
  32.6 1.9 %collective-permute-start.3 = (f32[3,8,384]{2,1,0:T(8,128)}, f32[3,8,384]{2,1,0:T(8,128)S(1)}, u32[]{:S(2)}, u32[]{:S(2)}) collective-permute-start(f32[3,8,384]{2,1,0:T(8,128)} %get-tuple-element.10), channel_id=1, source_target_pairs={{16,0},{32,16},{48,32},{64,48},{80,64},{96,80},{112,96},{128,112},... | collective-permute-start | bytes 110600 | tf_op jit(solution)/shard_map/ppermute | solution.py:121
  34.5 0.0 copy-done
  34.5 0.1 constant_dynamic-slice_fusion
  34.6 0.7 %copy.10 = f32[4,16]{0,1:T(8,128)} copy(f32[4,16]{1,0:T(4,128)S(1)} %constant_dynamic-slice_fusion) | data formatting | bytes 512
  35.3 0.0 collective-permute-done.2.up_ref
  35.3 0.0 copy-start.4
  35.3 6.1 %collective-permute-done.3.down_ref = f32[3,8,384]{2,1,0:T(8,128)S(1)} collective-permute-done((f32[3,8,384]{2,1,0:T(8,128)}, f32[3,8,384]{2,1,0:T(8,128)S(1)}, u32[]{:S(2)}, u32[]{:S(2)}) %collective-permute-start.3) | collective-permute-done | bytes 36896 | tf_op jit(solution)/shard_map/ppermute | solution.py:121
  41.4 0.0 copy-start.5
  41.4 0.0 copy-done.4
  41.4 0.6 %copy-done.5 = f32[3,8,384]{2,1,0:T(8,128)} copy-done((f32[3,8,384]{2,1,0:T(8,128)}, f32[3,8,384]{2,1,0:T(8,128)S(1)}, u32[]{:S(2)}) %copy-start.5) | copy-done | bytes 36888
  42.0 1.8 %shard_map.56 = f32[3,16,384]{2,1,0:T(8,128)} custom-call(f32[3,8,384]{2,1,0:T(8,128)} %copy-done.4, f32[3,16,384]{2,1,0:T(8,128)} %get-tuple-element.9.mid_ref, f32[3,8,384]{2,1,0:T(8,128)} %copy-done.5, s32[16,4]{1,0:T(8,128)} %iota_subtract_fusion.offs_ref, f32[16,4]{1,0:T(8,128)} %bitcast.14), custom_call_target="tpu_custom_call" | custom-call | tf_op jit(solution)/shard_map/pallas_call | solution.py:131
  (3 shorter events, 0.0 us)
Async XLA Ops:
  0.0 34.5 %copy-start = (f32[4,768]{1,0:T(4,128)S(1)}, f32[4,768]{1,0:T(4,128)}, u32[]{:S(2)}) copy-start(f32[4,768]{1,0:T(4,128)} %param.9) | copy-start | bytes 36868
  0.0 0.9 %copy-start.1 = (f32[3,1,16,384]{3,2,1,0:T(8,128)S(1)}, f32[3,1,16,384]{3,2,1,0:T(8,128)}, u32[]{:S(2)}) copy-start(f32[3,1,16,384]{3,2,1,0:T(8,128)} %param.5) | copy-start | bytes 221188
  1.0 0.7 %copy-start.7 = (s32[16]{0:T(128)S(1)}, s32[16]{0:T(128)}, u32[]{:S(2)}) copy-start(s32[16]{0:T(128)} %param.6) | copy-start | bytes 196
  1.7 13.6 %collective-permute-start = (f32[3,16,256]{2,1,0:T(8,128)S(1)}, f32[3,16,256]{2,1,0:T(8,128)S(1)}, u32[]{:S(2)}, u32[]{:S(2)}) collective-permute-start(f32[3,16,256]{2,1,0:T(8,128)S(1)} %slice_select_fusion), channel_id=1, source_target_pairs={{0,1},{1,0},{2,3},{3,2},{4,5},{5,4},{6,7},{7,6},{8,9},{9,8},{10,11... | collective-permute-start | bytes 147464 | tf_op jit(solution)/shard_map/ppermute | solution.py:104
  15.3 6.6 %copy-start.2 = (f32[3,16,256]{2,1,0:T(8,128)}, f32[3,16,256]{2,1,0:T(8,128)S(1)}, u32[]{:S(2)}) copy-start(f32[3,16,256]{2,1,0:T(8,128)S(1)} %collective-permute-done.p_ref) | copy-start | bytes 147460
  15.3 6.6 %collective-permute-start.1 = (f32[3,16,256]{2,1,0:T(8,128)S(1)}, f32[3,16,256]{2,1,0:T(8,128)S(1)}, u32[]{:S(2)}, u32[]{:S(2)}) collective-permute-start(f32[3,16,256]{2,1,0:T(8,128)S(1)} %collective-permute-done.p_ref), channel_id=1, source_target_pairs={{0,2},{1,15},{2,4},{3,1},{4,6},{5,3},{6,8},{7,5},{8,10},{9,7},{10,... | collective-permute-start | bytes 147464 | tf_op jit(solution)/shard_map/ppermute | solution.py:106
  18.6 0.7 %copy-start.6 = (f32[4,16]{1,0:T(4,128)S(1)}, f32[4,16]{1,0:T(4,128)}, u32[]{:S(2)}) copy-start(f32[4,16]{1,0:T(4,128)} %param.7) | copy-start | bytes 772
  21.9 0.6 %copy-start.3 = (f32[3,16,256]{2,1,0:T(8,128)}, f32[3,16,256]{2,1,0:T(8,128)S(1)}, u32[]{:S(2)}) copy-start(f32[3,16,256]{2,1,0:T(8,128)S(1)} %collective-permute-done.1.q_ref) | copy-start | bytes 147460
  24.9 10.4 %collective-permute-start.2 = (f32[3,8,384]{2,1,0:T(8,128)}, f32[3,8,384]{2,1,0:T(8,128)S(1)}, u32[]{:S(2)}, u32[]{:S(2)}) collective-permute-start(f32[3,8,384]{2,1,0:T(8,128)} %get-tuple-element.8), channel_id=1, source_target_pairs={{0,16},{16,32},{32,48},{48,64},{64,80},{80,96},{96,112},{112,128},... | collective-permute-start | bytes 110600 | tf_op jit(solution)/shard_map/ppermute | solution.py:120
  32.6 8.8 %collective-permute-start.3 = (f32[3,8,384]{2,1,0:T(8,128)}, f32[3,8,384]{2,1,0:T(8,128)S(1)}, u32[]{:S(2)}, u32[]{:S(2)}) collective-permute-start(f32[3,8,384]{2,1,0:T(8,128)} %get-tuple-element.10), channel_id=1, source_target_pairs={{16,0},{32,16},{48,32},{64,48},{80,64},{96,80},{112,96},{128,112},... | collective-permute-start | bytes 110600 | tf_op jit(solution)/shard_map/ppermute | solution.py:121
  35.3 6.1 %copy-start.4 = (f32[3,8,384]{2,1,0:T(8,128)}, f32[3,8,384]{2,1,0:T(8,128)S(1)}, u32[]{:S(2)}) copy-start(f32[3,8,384]{2,1,0:T(8,128)S(1)} %collective-permute-done.2.up_ref) | copy-start | bytes 110596
  41.4 0.6 %copy-start.5 = (f32[3,8,384]{2,1,0:T(8,128)}, f32[3,8,384]{2,1,0:T(8,128)S(1)}, u32[]{:S(2)}) copy-start(f32[3,8,384]{2,1,0:T(8,128)S(1)} %collective-permute-done.3.down_ref) | copy-start | bytes 110596

commit v7 on v6

--- a/solution.py
+++ b/solution.py
@@ -8,7 +8,6 @@
 LON_HALO = 256
 LAT_HALO = 8
 SHIFT_BITS = 9
-PACK_SHIFT = 64
 INTERPRET = False
 
 
@@ -38,13 +37,11 @@
     even_lon = par_ref[...] == 0
     base = offs_ref[...]
     w = [lw_ref[:, k:k + 1] for k in range(4)]
-    ahead = base < LON_HALO
     masks = [((base >> b) & 1) == 1 for b in range(SHIFT_BITS)]
     for t in range(tracers):
         p, q = p_ref[t], q_ref[t]
-        left = pltpu.roll(jnp.where(even_lon, q, p), PACK_SHIFT, 1)
+        left = jnp.where(even_lon, q, p)
         right = jnp.where(even_lon, p, q)
-        right = jnp.where(ahead, pltpu.roll(right, PACK_SHIFT, 1), right)
         row = jnp.concatenate([left, mid_ref[t], right], axis=1)
         for b in range(SHIFT_BITS):
             rolled = pltpu.roll(row, ext_width - (1 << b), 1)
@@ -94,13 +91,10 @@
     f32 = jnp.float32
     offs = lon_offsets.astype(jnp.int32)
     vmem, smem = pltpu.VMEM, pltpu.SMEM
-    tail = width - LON_HALO + PACK_SHIFT
-    ahead = (offs >= 0)[None, :, None]
-    packed = jnp.where(
-        ahead,
-        jnp.concatenate([block[:, :, tail:], block[:, :, :LON_HALO - width + tail]], axis=2),
-        block[:, :, :LON_HALO],
-    )
+    third = width // 3
+    lo = jnp.where((offs >= 2)[None, :, None], block[:, :, third:2 * third], block[:, :, :third])
+    hi = jnp.where((offs <= -1)[None, :, None], block[:, :, third:2 * third], block[:, :, 2 * third:])
+    packed = jnp.concatenate([lo, hi], axis=2)
     partner = lax.ppermute(packed, "lon", [(i, i ^ 1) for i in range(lon_count)])
     onward = [(i, (i + 2) % lon_count if i % 2 == 0 else (i - 2) % lon_count) for i in range(lon_count)]
     relayed = lax.ppermute(partner, "lon", onward)

time: 44.2 us -> 44 us (level)
  local copies, waits for them, and re-layouts: 4.93 us -> 3.35 us
  other arithmetic: 1.53 us -> 2.97 us
    slice x2 -> x0, local copies, waits for them, and re-layouts: 0.95 us -> none  [the longest x1 0.94 us: per_device(): block[:, :, tail:]]
    select_n x1, other arithmetic: 0.08 us -> 0.85 us  [per_device(): jnp.where((offs >= 2)[None, :, None], block[:, :, third:2 * third], block...]
    ge x1, other arithmetic: 0.01 us -> 0.67 us  [per_device(): offs >= 2]
    unnamed x18 -> x16, local copies, waits for them, and re-layouts: 3.23 us -> 2.6 us
where the time goes in v7:
time: 44 us; the launch traced here: 43.5 us
  starting transfers between devices  24.9 us (57%)
  waiting for transfers between devices  8.09 us (18%)
  Pallas kernels  4.08 us (9%)
  local copies, waits for them, and re-layouts  3.35 us (8%)
  other arithmetic  2.97 us (7%)
    ppermute x1, starting transfers between devices, per_device(): lax.ppermute(packed, 'lon', [(i, i ^ 1) for i in range(lon_count)])  12.2 us
    ppermute x1, starting transfers between devices, per_device(): up = lax.ppermute(bot, 'lat', down_pairs)  7.67 us
    ppermute x1, waiting for transfers between devices, per_device(): down = lax.ppermute(top, 'lat', up_pairs)  6.11 us
    ppermute x1, starting transfers between devices, per_device(): relayed = lax.ppermute(partner, 'lon', onward)  3.19 us
    unnamed x16, local copies, waits for them, and re-layouts  2.6 us
    pallas_call x1, Pallas kernels, per_device(): call(lon_kernel, (shape, halo, halo), [vmem] * 6)  2.27 us
    ppermute x1, waiting for transfers between devices, per_device(): relayed = lax.ppermute(partner, 'lon', onward)  1.97 us
    ppermute x1, starting transfers between devices, per_device(): down = lax.ppermute(top, 'lat', up_pairs)  1.92 us
  transfers between devices with their start and end apart: 4, of which 2 were waited for; matrix products, arithmetic and copies ran while one was open for 8% of the time, Pallas kernels for 0%

profile of v7, /device:TPU:199, one launch (start us, length us, event | category | flops | bytes accessed | tf_op | source)
XLA Modules:
  0.0 43.5 jit_solution(6114206074877558841)
XLA Ops:
  0.0 0.0 copy-start
  0.0 0.7 %broadcast_compare_fusion.1 = (pred[16]{0:T(512)(128)(4,1)S(1)}, pred[16]{0:T(512)(128)(4,1)S(1)}) fusion(s32[16]{0:T(128)} %param.6), kind=kLoop, calls=%fused_computation.8 | loop fusion | flops 32 | bytes 96 | tf_op jit(solution)/shard_map/ge | solution.py:95
  0.7 0.8 %slice_select_fusion.1 = (f32[3,16,128]{2,1,0:T(8,128)S(1)}, f32[3,16,128]{2,1,0:T(8,128)S(1)}) fusion(f32[3,16,384]{2,1,0:T(8,128)} %bitcast.9, pred[16]{0:T(512)(128)(4,1)S(1)} %get-tuple-element.13, pred[16]{0:T(512)(128)(4,1)S(1)} %get-tuple-element.14), kind=kLoop, calls=%fused_computation.2 | loop fusion | flops 12288 | bytes 122912 | tf_op jit(solution)/shard_map/jit(_where)/select_n | solution.py:95
  1.5 12.2 %collective-permute-start = (f32[3,16,256]{2,1,0:T(8,128)S(1)}, f32[3,16,256]{2,1,0:T(8,128)S(1)}, u32[]{:S(2)}, u32[]{:S(2)}) collective-permute-start(f32[3,16,256]{2,1,0:T(8,128)S(1)} %pad_maximum_fusion), channel_id=1, source_target_pairs={{0,1},{1,0},{2,3},{3,2},{4,5},{5,4},{6,7},{7,6},{8,9},{9,8},{10,11... | collective-permute-start | bytes 147464 | tf_op jit(solution)/shard_map/ppermute | solution.py:98
  13.7 0.8 %subtract_add_fusion = s32[16]{0:T(128)S(1)} fusion(s32[768]{0:T(1024)} %param.8, s32[]{:T(128)S(6)} %select_n.21, s32[]{:T(128)S(6)} %mul.3), kind=kLoop, calls=%fused_computation.4 | loop fusion | flops 48 | bytes 136 | tf_op jit(solution)/shard_map/sub | solution.py:123
  14.5 0.0 copy-start.6
  14.5 0.7 %iota_subtract_fusion.offs_ref = s32[16,4]{1,0:T(8,128)} fusion(s32[]{:T(128)S(6)} %mul.3, s32[16]{0:T(128)S(1)} %subtract_add_fusion), kind=kLoop, calls=%fused_computation.3 | loop fusion | flops 320 | bytes 324 | tf_op jit(solution)/shard_map/sub | solution.py:124
  15.2 0.0 collective-permute-done.p_ref
  15.2 0.0 copy-start.1
  15.2 3.2 %collective-permute-start.1 = (f32[3,16,256]{2,1,0:T(8,128)S(1)}, f32[3,16,256]{2,1,0:T(8,128)S(1)}, u32[]{:S(2)}, u32[]{:S(2)}) collective-permute-start(f32[3,16,256]{2,1,0:T(8,128)S(1)} %collective-permute-done.p_ref), channel_id=1, source_target_pairs={{0,2},{1,15},{2,4},{3,1},{4,6},{5,3},{6,8},{7,5},{8,10},{9,7},{10,... | collective-permute-start | bytes 147464 | tf_op jit(solution)/shard_map/ppermute | solution.py:100
  18.4 0.0 copy-done.6
  18.4 0.0 copy-start.5
  18.4 0.7 %copy.7.offs_ref = s32[16,1]{1,0:T(8,128)} copy(s32[16,1]{0,1:T(1,128)S(1)} %subtract_bitcast_fusion) | data formatting | bytes 128 | tf_op jit(solution)/shard_map/reshape | solution.py:105
  19.1 0.0 copy-done.5
  19.1 0.7 %copy.6 = f32[4,16]{0,1:T(8,128)} copy(f32[4,16]{1,0:T(4,128)S(1)} %copy-done.5) | data formatting | bytes 512 | tf_op args[2]
  19.8 2.0 %collective-permute-done.1.q_ref = f32[3,16,256]{2,1,0:T(8,128)S(1)} collective-permute-done((f32[3,16,256]{2,1,0:T(8,128)S(1)}, f32[3,16,256]{2,1,0:T(8,128)S(1)}, u32[]{:S(2)}, u32[]{:S(2)}) %collective-permute-start.1) | collective-permute-done | bytes 49184 | tf_op jit(solution)/shard_map/ppermute | solution.py:100
  21.7 0.0 copy-start.2
  21.7 0.0 copy-done.1
  21.7 0.6 %copy-done.2 = f32[3,16,256]{2,1,0:T(8,128)} copy-done((f32[3,16,256]{2,1,0:T(8,128)}, f32[3,16,256]{2,1,0:T(8,128)S(1)}, u32[]{:S(2)}) %copy-start.2) | copy-done | bytes 49176
  22.4 2.3 %shard_map.55 = (f32[3,16,384]{2,1,0:T(8,128)}, f32[3,8,384]{2,1,0:T(8,128)}, f32[3,8,384]{2,1,0:T(8,128)}) custom-call(f32[3,16,256]{2,1,0:T(8,128)} %copy-done.1, f32[3,16,384]{2,1,0:T(8,128)} %bitcast.10, f32[3,16,256]{2,1,0:T(8,128)} %copy-done.2, s32[1,1]{1,0:T(1,128)} %bitcast.1.par_ref, s32[16,1]{1,0:T(8,128)} %copy.7.offs_ref, f32[16,4]{1,0:T(8,128)} %bitcast.11), custom_call_target="tpu_custom_call" | custom-call | tf_op jit(solution)/shard_map/pallas_call | solution.py:107
  24.6 7.7 %collective-permute-start.2 = (f32[3,8,384]{2,1,0:T(8,128)}, f32[3,8,384]{2,1,0:T(8,128)S(1)}, u32[]{:S(2)}, u32[]{:S(2)}) collective-permute-start(f32[3,8,384]{2,1,0:T(8,128)} %get-tuple-element.8), channel_id=1, source_target_pairs={{0,16},{16,32},{32,48},{48,64},{64,80},{80,96},{96,112},{112,128},... | collective-permute-start | bytes 110600 | tf_op jit(solution)/shard_map/ppermute | solution.py:114
  32.3 1.9 %collective-permute-start.3 = (f32[3,8,384]{2,1,0:T(8,128)}, f32[3,8,384]{2,1,0:T(8,128)S(1)}, u32[]{:S(2)}, u32[]{:S(2)}) collective-permute-start(f32[3,8,384]{2,1,0:T(8,128)} %get-tuple-element.10), channel_id=1, source_target_pairs={{16,0},{32,16},{48,32},{64,48},{80,64},{96,80},{112,96},{128,112},... | collective-permute-start | bytes 110600 | tf_op jit(solution)/shard_map/ppermute | solution.py:115
  34.2 0.0 copy-done
  34.2 0.1 constant_dynamic-slice_fusion
  34.3 0.7 %copy.10 = f32[4,16]{0,1:T(8,128)} copy(f32[4,16]{1,0:T(4,128)S(1)} %constant_dynamic-slice_fusion) | data formatting | bytes 512
  35.0 0.0 collective-permute-done.2.up_ref
  35.0 0.0 copy-start.3
  35.0 6.1 %collective-permute-done.3.down_ref = f32[3,8,384]{2,1,0:T(8,128)S(1)} collective-permute-done((f32[3,8,384]{2,1,0:T(8,128)}, f32[3,8,384]{2,1,0:T(8,128)S(1)}, u32[]{:S(2)}, u32[]{:S(2)}) %collective-permute-start.3) | collective-permute-done | bytes 36896 | tf_op jit(solution)/shard_map/ppermute | solution.py:115
  41.1 0.0 copy-start.4
  41.1 0.0 copy-done.3
  41.1 0.6 %copy-done.4 = f32[3,8,384]{2,1,0:T(8,128)} copy-done((f32[3,8,384]{2,1,0:T(8,128)}, f32[3,8,384]{2,1,0:T(8,128)S(1)}, u32[]{:S(2)}) %copy-start.4) | copy-done | bytes 36888
  41.7 1.8 %shard_map.56 = f32[3,16,384]{2,1,0:T(8,128)} custom-call(f32[3,8,384]{2,1,0:T(8,128)} %copy-done.3, f32[3,16,384]{2,1,0:T(8,128)} %get-tuple-element.9.mid_ref, f32[3,8,384]{2,1,0:T(8,128)} %copy-done.4, s32[16,4]{1,0:T(8,128)} %iota_subtract_fusion.offs_ref, f32[16,4]{1,0:T(8,128)} %bitcast.12), custom_call_target="tpu_custom_call" | custom-call | tf_op jit(solution)/shard_map/pallas_call | solution.py:125
  (2 shorter events, 0.0 us)
Async XLA Ops:
  0.0 34.2 %copy-start = (f32[4,768]{1,0:T(4,128)S(1)}, f32[4,768]{1,0:T(4,128)}, u32[]{:S(2)}) copy-start(f32[4,768]{1,0:T(4,128)} %param.9) | copy-start | bytes 36868
  1.5 13.6 %collective-permute-start = (f32[3,16,256]{2,1,0:T(8,128)S(1)}, f32[3,16,256]{2,1,0:T(8,128)S(1)}, u32[]{:S(2)}, u32[]{:S(2)}) collective-permute-start(f32[3,16,256]{2,1,0:T(8,128)S(1)} %pad_maximum_fusion), channel_id=1, source_target_pairs={{0,1},{1,0},{2,3},{3,2},{4,5},{5,4},{6,7},{7,6},{8,9},{9,8},{10,11... | collective-permute-start | bytes 147464 | tf_op jit(solution)/shard_map/ppermute | solution.py:98
  14.5 3.9 %copy-start.6 = (s32[16]{0:T(128)S(1)}, s32[16]{0:T(128)}, u32[]{:S(2)}) copy-start(s32[16]{0:T(128)} %param.6) | copy-start | bytes 196
  15.2 6.6 %copy-start.1 = (f32[3,16,256]{2,1,0:T(8,128)}, f32[3,16,256]{2,1,0:T(8,128)S(1)}, u32[]{:S(2)}) copy-start(f32[3,16,256]{2,1,0:T(8,128)S(1)} %collective-permute-done.p_ref) | copy-start | bytes 147460
  15.2 6.6 %collective-permute-start.1 = (f32[3,16,256]{2,1,0:T(8,128)S(1)}, f32[3,16,256]{2,1,0:T(8,128)S(1)}, u32[]{:S(2)}, u32[]{:S(2)}) collective-permute-start(f32[3,16,256]{2,1,0:T(8,128)S(1)} %collective-permute-done.p_ref), channel_id=1, source_target_pairs={{0,2},{1,15},{2,4},{3,1},{4,6},{5,3},{6,8},{7,5},{8,10},{9,7},{10,... | collective-permute-start | bytes 147464 | tf_op jit(solution)/shard_map/ppermute | solution.py:100
  18.4 0.7 %copy-start.5 = (f32[4,16]{1,0:T(4,128)S(1)}, f32[4,16]{1,0:T(4,128)}, u32[]{:S(2)}) copy-start(f32[4,16]{1,0:T(4,128)} %param.7) | copy-start | bytes 772
  21.7 0.6 %copy-start.2 = (f32[3,16,256]{2,1,0:T(8,128)}, f32[3,16,256]{2,1,0:T(8,128)S(1)}, u32[]{:S(2)}) copy-start(f32[3,16,256]{2,1,0:T(8,128)S(1)} %collective-permute-done.1.q_ref) | copy-start | bytes 147460
  24.6 10.4 %collective-permute-start.2 = (f32[3,8,384]{2,1,0:T(8,128)}, f32[3,8,384]{2,1,0:T(8,128)S(1)}, u32[]{:S(2)}, u32[]{:S(2)}) collective-permute-start(f32[3,8,384]{2,1,0:T(8,128)} %get-tuple-element.8), channel_id=1, source_target_pairs={{0,16},{16,32},{32,48},{48,64},{64,80},{80,96},{96,112},{112,128},... | collective-permute-start | bytes 110600 | tf_op jit(solution)/shard_map/ppermute | solution.py:114
  32.3 8.8 %collective-permute-start.3 = (f32[3,8,384]{2,1,0:T(8,128)}, f32[3,8,384]{2,1,0:T(8,128)S(1)}, u32[]{:S(2)}, u32[]{:S(2)}) collective-permute-start(f32[3,8,384]{2,1,0:T(8,128)} %get-tuple-element.10), channel_id=1, source_target_pairs={{16,0},{32,16},{48,32},{64,48},{80,64},{96,80},{112,96},{128,112},... | collective-permute-start | bytes 110600 | tf_op jit(solution)/shard_map/ppermute | solution.py:115
  35.0 6.1 %copy-start.3 = (f32[3,8,384]{2,1,0:T(8,128)}, f32[3,8,384]{2,1,0:T(8,128)S(1)}, u32[]{:S(2)}) copy-start(f32[3,8,384]{2,1,0:T(8,128)S(1)} %collective-permute-done.2.up_ref) | copy-start | bytes 110596
  41.1 0.6 %copy-start.4 = (f32[3,8,384]{2,1,0:T(8,128)}, f32[3,8,384]{2,1,0:T(8,128)S(1)}, u32[]{:S(2)}) copy-start(f32[3,8,384]{2,1,0:T(8,128)S(1)} %collective-permute-done.3.down_ref) | copy-start | bytes 110596

commit v8 on v7

--- a/solution.py
+++ b/solution.py
@@ -55,21 +55,16 @@
         bot_ref[t] = total[rows - LAT_HALO:]
 
 
-def lat_kernel(up_ref, mid_ref, down_ref, offs_ref, lw_ref, out_ref):
+def lat_kernel(up_ref, mid_ref, down_ref, coef_ref, out_ref):
     tracers, rows, width = mid_ref.shape
     ext_rows = rows + 2 * LAT_HALO
-    d = [offs_ref[:, k:k + 1] for k in range(4)]
-    w = [lw_ref[:, k:k + 1] for k in range(4)]
+    coef = coef_ref[...]
     for t in range(tracers):
         ext = jnp.concatenate([up_ref[t], mid_ref[t], down_ref[t]], axis=0)
-        picks = [jnp.zeros((rows, width), jnp.float32) for _ in range(4)]
-        for s in range(LAT_HALO - 5, LAT_HALO + 7):
+        total = jnp.zeros((rows, width), jnp.float32)
+        for i, s in enumerate(range(LAT_HALO - 5, LAT_HALO + 7)):
             shifted = pltpu.roll(ext, ext_rows - s, 0)[:rows]
-            for k in range(4):
-                picks[k] = jnp.where(d[k] == s, shifted, picks[k])
-        total = jnp.zeros((rows, width), jnp.float32)
-        for k in range(4):
-            total = total + w[k] * picks[k]
+            total = total + coef[:, i:i + 1] * shifted
         out_ref[t] = total
 
 
@@ -122,9 +117,11 @@
     taps = jnp.arange(4, dtype=jnp.int32)
     source = jnp.clip(own[:, None] - lat_offs[:, None] - 1 + taps[None, :], 0, nlat - 1)
     d = (source - first + LAT_HALO - jnp.arange(rows, dtype=jnp.int32)[:, None]).astype(jnp.int32)
-    out = call(lat_kernel, shape, [vmem] * 5)(
-        up, swept, down, d, jnp.transpose(lat_w).astype(f32)
-    )
+    shifts = jnp.arange(LAT_HALO - 5, LAT_HALO + 7, dtype=jnp.int32)
+    hits = (d[:, :, None] == shifts[None, None, :]).astype(f32)
+    coef = jnp.einsum("jk,jks->js", jnp.transpose(lat_w).astype(f32), hits,
+                      precision=lax.Precision.HIGHEST)
+    out = call(lat_kernel, shape, [vmem] * 4)(up, swept, down, coef)
     return out.reshape(tracers.shape)
 
 

time: 44 us -> 43.8 us (level)
  matrix products: 0 us -> 0.85 us
  other arithmetic: 2.97 us -> 2.38 us
  local copies, waits for them, and re-layouts: 3.35 us -> 2.76 us
    dot_general x0 -> x1, matrix products: none -> 0.85 us  [per_device(): jnp.einsum('jk,jks->js', jnp.transpose(lat_w).astype(f32), hits, precisio...]
    unnamed x16 -> x15, local copies, waits for them, and re-layouts: 2.6 us -> 1.92 us
    sub x1, other arithmetic: 0.67 us -> 0.08 us  [per_device(): source - first + LAT_HALO - jnp.arange(rows, dtype=jnp.int32)[:, None]]
    ppermute x1, waiting for transfers between devices: 0.01 us -> 0.49 us  [per_device(): lax.ppermute(packed, 'lon', [(i, i ^ 1) for i in range(lon_count)])]
  transfers between devices with their start and end apart: 4 -> 4, of which waited for: 2 -> 3; matrix products, arithmetic and copies ran while one was open for 8% -> 7% of each run, Pallas kernels for 0% -> 0%
where the time goes in v8:
time: 43.8 us; the launch traced here: 43.4 us
  starting transfers between devices  24.9 us (57%)
  waiting for transfers between devices  8.42 us (19%)
  Pallas kernels  3.93 us (9%)
  local copies, waits for them, and re-layouts  2.76 us (6%)
  other arithmetic  2.38 us (5%)
  matrix products  0.85 us (2%)
    ppermute x1, starting transfers between devices, per_device(): lax.ppermute(packed, 'lon', [(i, i ^ 1) for i in range(lon_count)])  12.2 us
    ppermute x1, starting transfers between devices, per_device(): up = lax.ppermute(bot, 'lat', down_pairs)  7.67 us
    ppermute x1, waiting for transfers between devices, per_device(): down = lax.ppermute(top, 'lat', up_pairs)  6.02 us
    ppermute x1, starting transfers between devices, per_device(): relayed = lax.ppermute(partner, 'lon', onward)  3.19 us
    pallas_call x1, Pallas kernels, per_device(): call(lon_kernel, (shape, halo, halo), [vmem] * 6)  2.27 us
    unnamed x15, local copies, waits for them, and re-layouts  1.92 us
    ppermute x1, starting transfers between devices, per_device(): down = lax.ppermute(top, 'lat', up_pairs)  1.92 us
    ppermute x1, waiting for transfers between devices, per_device(): relayed = lax.ppermute(partner, 'lon', onward)  1.89 us
  transfers between devices with their start and end apart: 4, of which 3 were waited for; matrix products, arithmetic and copies ran while one was open for 7% of the time, Pallas kernels for 0%

profile of v8, /device:TPU:199, one launch (start us, length us, event | category | flops | bytes accessed | tf_op | source)
XLA Modules:
  0.0 43.4 jit_solution(1665502952848188015)
XLA Ops:
  0.0 0.0 copy-start
  0.0 0.7 %broadcast_compare_fusion.1 = (pred[16]{0:T(512)(128)(4,1)S(1)}, pred[16]{0:T(512)(128)(4,1)S(1)}) fusion(s32[16]{0:T(128)} %param.6), kind=kLoop, calls=%fused_computation.13 | loop fusion | flops 32 | bytes 96 | tf_op jit(solution)/shard_map/ge | solution.py:90
  0.7 0.8 %slice_select_fusion.1 = (f32[3,16,128]{2,1,0:T(8,128)S(1)}, f32[3,16,128]{2,1,0:T(8,128)S(1)}) fusion(f32[3,16,384]{2,1,0:T(8,128)} %bitcast.15, pred[16]{0:T(512)(128)(4,1)S(1)} %get-tuple-element.13, pred[16]{0:T(512)(128)(4,1)S(1)} %get-tuple-element.14), kind=kLoop, calls=%fused_computation.4 | loop fusion | flops 12288 | bytes 122912 | tf_op jit(solution)/shard_map/jit(_where)/select_n | solution.py:90
  1.5 0.0 copy-start.6
  1.5 12.2 %collective-permute-start = (f32[3,16,256]{2,1,0:T(8,128)S(1)}, f32[3,16,256]{2,1,0:T(8,128)S(1)}, u32[]{:S(2)}, u32[]{:S(2)}) collective-permute-start(f32[3,16,256]{2,1,0:T(8,128)S(1)} %pad_maximum_fusion), channel_id=1, source_target_pairs={{0,1},{1,0},{2,3},{3,2},{4,5},{5,4},{6,7},{7,6},{8,9},{9,8},{10,11... | collective-permute-start | bytes 147464 | tf_op jit(solution)/shard_map/ppermute | solution.py:93
  13.7 0.0 copy-done.6
  13.8 0.8 %subtract_add_fusion = s32[16]{0:T(128)S(1)} fusion(s32[768]{0:T(1024)} %param.8, s32[]{:T(128)S(6)} %select_n.21, s32[]{:T(128)S(6)} %mul.3), kind=kLoop, calls=%fused_computation.10 | loop fusion | flops 48 | bytes 136 | tf_op jit(solution)/shard_map/sub | solution.py:118
  14.5 0.1 iota_subtract_fusion
  14.6 0.0 copy-done
  14.6 0.1 dynamic-slice_bitcast_fusion
  14.7 0.5 %collective-permute-done.p_ref = f32[3,16,256]{2,1,0:T(8,128)S(1)} collective-permute-done((f32[3,16,256]{2,1,0:T(8,128)S(1)}, f32[3,16,256]{2,1,0:T(8,128)S(1)}, u32[]{:S(2)}, u32[]{:S(2)}) %collective-permute-start) | collective-permute-done | bytes 49184 | tf_op jit(solution)/shard_map/ppermute | solution.py:93
  15.2 0.0 copy-start.1
  15.2 3.2 %collective-permute-start.1 = (f32[3,16,256]{2,1,0:T(8,128)S(1)}, f32[3,16,256]{2,1,0:T(8,128)S(1)}, u32[]{:S(2)}, u32[]{:S(2)}) collective-permute-start(f32[3,16,256]{2,1,0:T(8,128)S(1)} %collective-permute-done.p_ref), channel_id=1, source_target_pairs={{0,2},{1,15},{2,4},{3,1},{4,6},{5,3},{6,8},{7,5},{8,10},{9,7},{10,... | collective-permute-start | bytes 147464 | tf_op jit(solution)/shard_map/ppermute | solution.py:95
  18.4 0.0 copy-start.5
  18.4 0.7 %copy.7.offs_ref = s32[16,1]{1,0:T(8,128)} copy(s32[16,1]{0,1:T(1,128)S(1)} %subtract_bitcast_fusion) | data formatting | bytes 128 | tf_op jit(solution)/shard_map/reshape | solution.py:100
  19.1 0.0 copy-done.5
  19.1 0.7 %copy.6 = f32[4,16]{0,1:T(8,128)} copy(f32[4,16]{1,0:T(4,128)S(1)} %copy-done.5) | data formatting | bytes 512 | tf_op args[2]
  19.8 0.1 copy.9
  19.8 1.9 %collective-permute-done.1.q_ref = f32[3,16,256]{2,1,0:T(8,128)S(1)} collective-permute-done((f32[3,16,256]{2,1,0:T(8,128)S(1)}, f32[3,16,256]{2,1,0:T(8,128)S(1)}, u32[]{:S(2)}, u32[]{:S(2)}) %collective-permute-start.1) | collective-permute-done | bytes 49184 | tf_op jit(solution)/shard_map/ppermute | solution.py:95
  21.7 0.0 copy-start.2
  21.7 0.0 copy-done.1
  21.7 0.6 %copy-done.2 = f32[3,16,256]{2,1,0:T(8,128)} copy-done((f32[3,16,256]{2,1,0:T(8,128)}, f32[3,16,256]{2,1,0:T(8,128)S(1)}, u32[]{:S(2)}) %copy-start.2) | copy-done | bytes 49176
  22.4 2.3 %shard_map.55 = (f32[3,16,384]{2,1,0:T(8,128)}, f32[3,8,384]{2,1,0:T(8,128)}, f32[3,8,384]{2,1,0:T(8,128)}) custom-call(f32[3,16,256]{2,1,0:T(8,128)} %copy-done.1, f32[3,16,384]{2,1,0:T(8,128)} %bitcast.16, f32[3,16,256]{2,1,0:T(8,128)} %copy-done.2, s32[1,1]{1,0:T(1,128)} %bitcast.1.par_ref, s32[16,1]{1,0:T(8,128)} %copy.7.offs_ref, f32[16,4]{1,0:T(8,128)} %bitcast.17), custom_call_target="tpu_custom_call" | custom-call | tf_op jit(solution)/shard_map/pallas_call | solution.py:102
  24.6 7.7 %collective-permute-start.2 = (f32[3,8,384]{2,1,0:T(8,128)}, f32[3,8,384]{2,1,0:T(8,128)S(1)}, u32[]{:S(2)}, u32[]{:S(2)}) collective-permute-start(f32[3,8,384]{2,1,0:T(8,128)} %get-tuple-element.8), channel_id=1, source_target_pairs={{0,16},{16,32},{32,48},{48,64},{64,80},{80,96},{96,112},{112,128},... | collective-permute-start | bytes 110600 | tf_op jit(solution)/shard_map/ppermute | solution.py:109
  32.3 1.9 %collective-permute-start.3 = (f32[3,8,384]{2,1,0:T(8,128)}, f32[3,8,384]{2,1,0:T(8,128)S(1)}, u32[]{:S(2)}, u32[]{:S(2)}) collective-permute-start(f32[3,8,384]{2,1,0:T(8,128)} %get-tuple-element.10), channel_id=1, source_target_pairs={{16,0},{32,16},{48,32},{64,48},{80,64},{96,80},{112,96},{128,112},... | collective-permute-start | bytes 110600 | tf_op jit(solution)/shard_map/ppermute | solution.py:110
  34.2 0.8 %fusion = f32[16,1,12]{2,1,0:T(1,128)} fusion(f32[16,4,1]{1,2,0:T(1,128)S(1)} %copy.9, s32[12]{0:T(128)S(1)} %iota_add_fusion, s32[16,4]{1,0:T(8,128)S(1)} %iota_subtract_fusion), kind=kOutput, calls=%fused_computation.1 | convolution fusion | flops 9984 | bytes 1328 | tf_op jit(solution)/shard_map/jk,jks->js/dot_general | solution.py:122
  35.1 0.0 collective-permute-done.2.up_ref
  35.1 0.0 copy-start.3
  35.1 6.0 %collective-permute-done.3.down_ref = f32[3,8,384]{2,1,0:T(8,128)S(1)} collective-permute-done((f32[3,8,384]{2,1,0:T(8,128)}, f32[3,8,384]{2,1,0:T(8,128)S(1)}, u32[]{:S(2)}, u32[]{:S(2)}) %collective-permute-start.3) | collective-permute-done | bytes 36896 | tf_op jit(solution)/shard_map/ppermute | solution.py:110
  41.1 0.0 copy-start.4
  41.1 0.0 copy-done.3
  41.1 0.6 %copy-done.4 = f32[3,8,384]{2,1,0:T(8,128)} copy-done((f32[3,8,384]{2,1,0:T(8,128)}, f32[3,8,384]{2,1,0:T(8,128)S(1)}, u32[]{:S(2)}) %copy-start.4) | copy-done | bytes 36888
  41.7 1.7 %shard_map.56 = f32[3,16,384]{2,1,0:T(8,128)} custom-call(f32[3,8,384]{2,1,0:T(8,128)} %copy-done.3, f32[3,16,384]{2,1,0:T(8,128)} %get-tuple-element.9.mid_ref, f32[3,8,384]{2,1,0:T(8,128)} %copy-done.4, f32[16,12]{1,0:T(8,128)} %bitcast.18), custom_call_target="tpu_custom_call" | custom-call | tf_op jit(solution)/shard_map/pallas_call | solution.py:124
  (3 shorter events, 0.0 us)
Async XLA Ops:
  0.0 14.6 %copy-start = (f32[4,768]{1,0:T(4,128)S(1)}, f32[4,768]{1,0:T(4,128)}, u32[]{:S(2)}) copy-start(f32[4,768]{1,0:T(4,128)} %param.9) | copy-start | bytes 36868
  1.5 12.2 %copy-start.6 = (s32[16]{0:T(128)S(1)}, s32[16]{0:T(128)}, u32[]{:S(2)}) copy-start(s32[16]{0:T(128)} %param.6) | copy-start | bytes 196
  1.5 13.6 %collective-permute-start = (f32[3,16,256]{2,1,0:T(8,128)S(1)}, f32[3,16,256]{2,1,0:T(8,128)S(1)}, u32[]{:S(2)}, u32[]{:S(2)}) collective-permute-start(f32[3,16,256]{2,1,0:T(8,128)S(1)} %pad_maximum_fusion), channel_id=1, source_target_pairs={{0,1},{1,0},{2,3},{3,2},{4,5},{5,4},{6,7},{7,6},{8,9},{9,8},{10,11... | collective-permute-start | bytes 147464 | tf_op jit(solution)/shard_map/ppermute | solution.py:93
  15.2 6.6 %copy-start.1 = (f32[3,16,256]{2,1,0:T(8,128)}, f32[3,16,256]{2,1,0:T(8,128)S(1)}, u32[]{:S(2)}) copy-start(f32[3,16,256]{2,1,0:T(8,128)S(1)} %collective-permute-done.p_ref) | copy-start | bytes 147460
  15.2 6.6 %collective-permute-start.1 = (f32[3,16,256]{2,1,0:T(8,128)S(1)}, f32[3,16,256]{2,1,0:T(8,128)S(1)}, u32[]{:S(2)}, u32[]{:S(2)}) collective-permute-start(f32[3,16,256]{2,1,0:T(8,128)S(1)} %collective-permute-done.p_ref), channel_id=1, source_target_pairs={{0,2},{1,15},{2,4},{3,1},{4,6},{5,3},{6,8},{7,5},{8,10},{9,7},{10,... | collective-permute-start | bytes 147464 | tf_op jit(solution)/shard_map/ppermute | solution.py:95
  18.4 0.7 %copy-start.5 = (f32[4,16]{1,0:T(4,128)S(1)}, f32[4,16]{1,0:T(4,128)}, u32[]{:S(2)}) copy-start(f32[4,16]{1,0:T(4,128)} %param.7) | copy-start | bytes 772
  21.7 0.6 %copy-start.2 = (f32[3,16,256]{2,1,0:T(8,128)}, f32[3,16,256]{2,1,0:T(8,128)S(1)}, u32[]{:S(2)}) copy-start(f32[3,16,256]{2,1,0:T(8,128)S(1)} %collective-permute-done.1.q_ref) | copy-start | bytes 147460
  24.6 10.5 %collective-permute-start.2 = (f32[3,8,384]{2,1,0:T(8,128)}, f32[3,8,384]{2,1,0:T(8,128)S(1)}, u32[]{:S(2)}, u32[]{:S(2)}) collective-permute-start(f32[3,8,384]{2,1,0:T(8,128)} %get-tuple-element.8), channel_id=1, source_target_pairs={{0,16},{16,32},{32,48},{48,64},{64,80},{80,96},{96,112},{112,128},... | collective-permute-start | bytes 110600 | tf_op jit(solution)/shard_map/ppermute | solution.py:109
  32.3 8.8 %collective-permute-start.3 = (f32[3,8,384]{2,1,0:T(8,128)}, f32[3,8,384]{2,1,0:T(8,128)S(1)}, u32[]{:S(2)}, u32[]{:S(2)}) collective-permute-start(f32[3,8,384]{2,1,0:T(8,128)} %get-tuple-element.10), channel_id=1, source_target_pairs={{16,0},{32,16},{48,32},{64,48},{80,64},{96,80},{112,96},{128,112},... | collective-permute-start | bytes 110600 | tf_op jit(solution)/shard_map/ppermute | solution.py:110
  35.1 6.0 %copy-start.3 = (f32[3,8,384]{2,1,0:T(8,128)}, f32[3,8,384]{2,1,0:T(8,128)S(1)}, u32[]{:S(2)}) copy-start(f32[3,8,384]{2,1,0:T(8,128)S(1)} %collective-permute-done.2.up_ref) | copy-start | bytes 110596
  41.1 0.6 %copy-start.4 = (f32[3,8,384]{2,1,0:T(8,128)}, f32[3,8,384]{2,1,0:T(8,128)S(1)}, u32[]{:S(2)}) copy-start(f32[3,8,384]{2,1,0:T(8,128)S(1)} %collective-permute-done.3.down_ref) | copy-start | bytes 110596
